TPU v7x, 256 devices: a whole 4x4x8 slice. The times are simulated.
256 devices in a mesh: view: 16 (over z, y_hi), row: 16 (over x, y_lo, core).
Axes of the slice: x: 4, y: 4 (y_hi: 2, y_lo: 2; y = y_hi * 2 + y_lo), z: 8, core: 2. Of those that a mesh axis runs over, the one named last changes fastest.
Arguments:
- latent: bfloat16 [1, 16, 32, 72, 1280], P(None, 'view', 'row'), may hold values from -30 to 30
- gn_gain: float32 [1280], replicated, may hold values from 0.25 to 1.75
- gn_bias: float32 [1280], replicated, may hold values from -3 to 3
- cam_idx: int32 [1, 16], P(None, 'view'), may hold values from 0 to 63
- noise_idx: int32 [1], replicated, may hold values from 0 to 999
- cam_table: bfloat16 [64, 2560], replicated, may hold values from -2 to 2
- noise_table: bfloat16 [1000, 2560], replicated, may hold values from -2 to 2
- conv_w: bfloat16 [3, 3, 1280, 1280], P(None, None, None, 'row'), may hold values from -0.0546875 to 0.0546875
- conv_bias: float32 [1280], replicated, may hold values from -3 to 3
- ln_gain: float32 [1280], replicated, may hold values from 0.25 to 1.75
- attn_in: bfloat16 [3, 1280, 1280], P(None, None, 'view'), may hold values from -0.15625 to 0.15625
- attn_out: bfloat16 [1280, 1280], P('view'), may hold values from -0.15625 to 0.15625
- head_scale: float32 [20], replicated, may hold values from 0.4 to 135
Outputs:
- block_out: bfloat16 [1, 16, 32, 72, 1280], P(None, 'view', 'row')
All inputs are finite; a program needn't handle non-finite values.
Results may differ from a plain program's by a relative error of at most 0.02.
Values may be sent and summed in bfloat16 or wider, within the bound.
No kernel may reach another device: no remote copies, remote signals or barrier semaphores. Data moves between devices by JAX's collectives and lax.ppermute only.
A program may use at most 192 MiB of HBM per device.

v0:
```python
import math

import jax
import jax.numpy as jnp
from jax import lax
from jax.sharding import PartitionSpec as P

GROUPS = 32


epsilon = 1e-05


def convolve(padded, weight, out_rows, out_cols):
    channels = padded.shape[-1]
    summed = jnp.zeros(
        (padded.shape[0] * padded.shape[1] * out_rows * out_cols, weight.shape[-1]), jnp.float32
    )
    for tap_row in range(3):
        for tap_col in range(3):
            tap_rows = padded[
                :, :, tap_row : tap_row + out_rows, tap_col : tap_col + out_cols, :
            ].reshape(-1, channels)
            summed = summed + jnp.dot(
                tap_rows, weight[tap_row, tap_col], preferred_element_type=jnp.float32
            )
    return summed.reshape(padded.shape[0], padded.shape[1], out_rows, out_cols, weight.shape[-1])


def attend(query, key_block, value, head_scale):
    view_count = query.shape[0]
    item_count = query.shape[2]
    channels = query.shape[3]
    head_count = head_scale.shape[0]
    head_size = channels // head_count
    query_heads = query.reshape(view_count, item_count, head_count, head_size)
    key_heads = key_block.reshape(view_count, item_count, head_count, head_size)
    value_heads = value.reshape(view_count, item_count, head_count, head_size)
    scores = jnp.einsum(
        "vihd,uihd->ihvu", query_heads, key_heads, preferred_element_type=jnp.float32
    )
    scores = scores * (head_scale / math.sqrt(head_size))[None, :, None, None]
    peak_score = jnp.max(scores, axis=-1, keepdims=True)
    exp_scores = jnp.exp(scores - peak_score)
    soft_weights = (exp_scores / jnp.sum(exp_scores, axis=-1, keepdims=True)).astype(jnp.bfloat16)
    mixed = jnp.einsum(
        "ihvu,uihd->vihd", soft_weights, value_heads, preferred_element_type=jnp.float32
    )
    return mixed.astype(jnp.bfloat16).reshape(view_count, 1, item_count, channels)


def send_back(mixed):
    return lax.all_to_all(mixed, "view", split_axis=0, concat_axis=1, tiled=True)


def local(
    latent,
    gn_gain,
    gn_bias,
    cam_idx,
    noise_idx,
    cam_table,
    noise_table,
    conv_w,
    conv_bias,
    ln_gain,
    attn_in,
    attn_out,
    head_scale,
):
    samples, local_views, local_rows, local_cols, channels = latent.shape
    width_out = ln_gain.shape[0]
    x_float = latent.astype(jnp.float32)
    grouped = x_float.reshape(
        samples, local_views, local_rows, local_cols, GROUPS, channels // GROUPS
    )
    entries = local_rows * local_cols * (channels // GROUPS) * lax.axis_size("row")
    summed = lax.psum(jnp.sum(grouped, axis=(2, 3, 5)), "row")
    average = (summed / entries)[:, :, None, None, :, None]
    centred = grouped - average
    spread = lax.psum(jnp.sum(centred * centred, axis=(2, 3, 5)), "row")
    variance = (spread / entries)[:, :, None, None, :, None]
    normed = (centred * lax.rsqrt(variance + epsilon)).reshape(x_float.shape)
    cam_hot = (cam_idx[:, :, None] == jnp.arange(cam_table.shape[0], dtype=jnp.int32)).astype(
        jnp.bfloat16
    )
    cam_film = jnp.einsum("svn,nc->svc", cam_hot, cam_table, preferred_element_type=jnp.float32)
    noise_hot = (noise_idx[:, None] == jnp.arange(noise_table.shape[0], dtype=jnp.int32)).astype(
        jnp.bfloat16
    )
    noise_film = jnp.dot(noise_hot, noise_table, preferred_element_type=jnp.float32)
    film_rows = cam_film + noise_film[:, None, :]
    film_scale = film_rows[:, :, None, None, :channels]
    film_shift = film_rows[:, :, None, None, channels:]
    hidden = (normed * gn_gain + gn_bias) * (1.0 + film_scale) + film_shift
    activated = jax.nn.silu(hidden).astype(jnp.bfloat16)
    all_rows_act = lax.all_gather(activated, "row", axis=2, tiled=True)
    padded = jnp.pad(all_rows_act, ((0, 0), (0, 0), (1, 1), (1, 1), (0, 0)))
    partial_out = convolve(padded, conv_w, all_rows_act.shape[2], local_cols)
    conv_out = lax.all_to_all(partial_out, "row", split_axis=2, concat_axis=4, tiled=True)
    resid_out = (x_float + conv_out + conv_bias).astype(jnp.bfloat16)
    resid_float = resid_out.astype(jnp.float32)
    middle = jnp.mean(resid_float, axis=-1, keepdims=True)
    spread_y = jnp.mean((resid_float - middle) ** 2, axis=-1, keepdims=True)
    normed_y = ((resid_float - middle) * lax.rsqrt(spread_y + epsilon) * ln_gain).astype(
        jnp.bfloat16
    )
    weights_in = lax.all_gather(attn_in, "view", axis=2, tiled=True)
    view_devices = lax.axis_size("view")
    per_device = samples * local_rows * local_cols // view_devices
    pixel_major = jnp.moveaxis(normed_y, 1, 0).reshape(
        local_views, view_devices, per_device, width_out
    )

    def project(pixel_block, matrix_index):
        block_shape = pixel_block.shape
        flat_block = pixel_block.reshape(-1, width_out)
        return (
            jnp.dot(flat_block, weights_in[matrix_index], preferred_element_type=jnp.float32)
            .astype(jnp.bfloat16)
            .reshape(block_shape)
        )

    triple_in = (project(pixel_major, 0), project(pixel_major, 1), project(pixel_major, 2))
    mixed = send_back(
        attend(
            lax.all_to_all(triple_in[0], "view", split_axis=1, concat_axis=0, tiled=True),
            lax.all_to_all(triple_in[1], "view", split_axis=1, concat_axis=0, tiled=True),
            lax.all_to_all(triple_in[2], "view", split_axis=1, concat_axis=0, tiled=True),
            head_scale,
        )
    )
    mixed = jnp.moveaxis(
        mixed.reshape(local_views, samples, local_rows, local_cols, width_out), 0, 1
    )
    flat_mixed = mixed.reshape(-1, width_out)
    projected = jnp.dot(
        flat_mixed,
        lax.all_gather(attn_out, "view", axis=0, tiled=True),
        preferred_element_type=jnp.float32,
    )
    return (resid_float + projected.reshape(resid_float.shape)).astype(jnp.bfloat16)


def solution(mesh):
    placed = (
        P(None, "view", "row", None, None),
        P(),
        P(),
        P(None, "view"),
        P(),
        P(),
        P(),
        P(None, None, None, "row"),
        P(),
        P(),
        P(None, None, "view"),
        P("view", None),
        P(),
    )
    return jax.shard_map(
        local,
        mesh=mesh,
        in_specs=placed,
        out_specs=P(None, "view", "row", None, None),
        check_vma=False,
    )
```

profile of v0, /device:TPU:1, one launch (start us, length us, event | category | flops | bytes accessed | tf_op | source)
XLA Modules:
  0.0 409.2 jit_solution(9763920457493276366)
XLA Ops:
  6.6 1.1 convert_reduce_fusion.1
  7.9 29.7 %psum.14 = f32[1,1,32]{2,1,0:T(1,128)S(1)} all-reduce(f32[1,1,32]{2,1,0:T(1,128)S(1)} %bitcast.140), channel_id=1, replica_groups=mesh['view'=16,'row'=16] {'row'}, use_global_device_ids=true, to_apply=%region_2.0 | all-reduce | flops 32 | bytes 256 | tf_op jit(solution)/shard_map/psum | solution.py:78
  37.8 1.1 fusion.28
  39.1 28.6 %psum.15 = f32[1,1,32]{2,1,0:T(1,128)S(1)} all-reduce(f32[1,1,32]{2,1,0:T(1,128)S(1)} %bitcast.139), channel_id=1, replica_groups=mesh['view'=16,'row'=16] {'row'}, use_global_device_ids=true, to_apply=%region_5.6 | all-reduce | flops 32 | bytes 256 | tf_op jit(solution)/shard_map/psum | solution.py:81
  69.2 3.2 convolution_reduce_fusion
  75.3 42.8 %all-gather.4.cloned.1.call-done = bf16[1,1,32,72,1280]{4,3,1,0,2:T(8,128)(2,1)} async-done(((bf16[1,1,2,72,1280]{4,3,1,0,2:T(8,128)(2,1)}), bf16[1,1,32,72,1280]{4,3,1,0,2:T(8,128)(2,1)}) %all-gather.4.cloned.1.call-update) | async-done | bytes 5898256 | tf_op jit(solution)/shard_map/all_gather | solution.py:97
  118.1 35.5 %pad_slice_fusion = (bf16[1,1,32,72,1280]{4,3,1,0,2:T(8,128)(2,1)S(1)}, bf16[1,1,32,72,1280]{4,3,1,0,2:T(8,128)(2,1)}, bf16[1,1,32,72,1280]{4,3,1,0,2:T(8,128)(2...) fusion(bf16[1,1,32,72,1280]{4,3,1,0,2:T(8,128)(2,1)} %all-gathe, ...), kind=kLoop, calls=%fused_computation.1 | loop fusion | bytes 53084160 | tf_op jit(solution)/shard_map/slice | solution.py:21
  153.6 4.8 %fusion.48 = f32[2304,80]{0,1:T(8,128)S(1)} fusion(bf16[2304,1280]{1,0:T(8,128)(2,1)} %bitcast.132, bf16[3,3,1280,80]{2,3,1,0:T(8,128)(2,1)S(1)} %copy-done.4), kind=kOutput, calls=%fused_computation.73 | convolution fusion | flops 471859200 | bytes 6840320 | tf_op jit(solution)/shard_map/dot_general | solution.py:24
  158.4 4.8 %convolution_add_fusion.7 = f32[2304,80]{0,1:T(8,128)S(1)} fusion(f32[2304,80]{0,1:T(8,128)S(1)} %fusion.48, bf16[2304,1280]{1,0:T(8,128)(2,1)} %bitcast.131, bf16[3,3,1280,80]{2,3,1,0:T(8,128)(2,1)S(1)} %copy-done.4), kind=kOutput, calls=%fused_computation.16 | convolution fusion | flops 472043520 | bytes 7577600 | tf_op jit(solution)/shard_map/dot_general | solution.py:24
  163.2 1.9 convolution_add_fusion.6
  165.2 1.9 convolution_add_fusion.5
  167.3 1.9 convolution_add_fusion.4
  169.3 1.9 convolution_add_fusion.3
  171.4 1.9 convolution_add_fusion.2
  173.4 1.9 convolution_add_fusion.1
  175.3 2.9 convolution_add_fusion
  178.6 23.5 %all_to_all.54 = f32[1,1,32,72,80]{4,3,1,0,2:T(8,128)S(1)} all-to-all(f32[1,1,32,72,80]{4,3,1,0,2:T(8,128)S(1)} %bitcast.134), channel_id=1, replica_groups=mesh['view'=16,'row'=16] {'row'}, dimensions={2} | all-to-all | bytes 1474560 | tf_op jit(solution)/shard_map/all_to_all | solution.py:100
  203.7 79.4 %all-gather.6.cloned.1.call-done = bf16[3,1280,1280]{1,2,0:T(8,128)(2,1)} async-done(((bf16[3,1280,80]{1,2,0:T(8,128)(2,1)}), bf16[3,1280,1280]{1,2,0:T(8,128)(2,1)}) %all-gather.6.cloned.1.call-update) | async-done | bytes 9830416 | tf_op jit(solution)/shard_map/all_gather | solution.py:108
  283.1 3.1 fusion.16
  287.2 4.2 %all-to-all-start.2 = ((bf16[1,16,9,1280]{3,2,0,1:T(8,128)(2,1)}), bf16[1,16,9,1280]{3,2,0,1:T(8,128)(2,1)S(1)}, u32[]{:S(2)}, u32[]{:S(2)}) async-start(bf16[1,16,9,1280]{3,2,0,1:T(8,128)(2,1)} %bitcast.33), calls=%async_computation.2 | async-start | bytes 1310720 | tf_op jit(solution)/shard_map/all_to_all | solution.py:127
  291.4 3.2 fusion.17
  295.6 18.2 %all-to-all-done.2 = bf16[1,16,9,1280]{3,2,0,1:T(8,128)(2,1)S(1)} async-done(((bf16[1,16,9,1280]{3,2,0,1:T(8,128)(2,1)}), bf16[1,16,9,1280]{3,2,0,1:T(8,128)(2,1)S(1)}, u32[]{:S(2)}, u32[]{:S(2)}) %all-to-all-start.2) | async-done | bytes 368672 | tf_op jit(solution)/shard_map/all_to_all | solution.py:127
  313.7 5.1 %all-to-all-start.3 = ((bf16[1,16,9,1280]{3,2,0,1:T(8,128)(2,1)}), bf16[1,16,9,1280]{3,2,0,1:T(8,128)(2,1)S(1)}, u32[]{:S(2)}, u32[]{:S(2)}) async-start(bf16[1,16,9,1280]{3,2,0,1:T(8,128)(2,1)} %bitcast.35), calls=%async_computation.3 | async-start | bytes 1310720 | tf_op jit(solution)/shard_map/all_to_all | solution.py:128
  318.8 3.2 fusion.15
  323.0 15.5 %all-to-all-done.3 = bf16[1,16,9,1280]{3,2,0,1:T(8,128)(2,1)S(1)} async-done(((bf16[1,16,9,1280]{3,2,0,1:T(8,128)(2,1)}), bf16[1,16,9,1280]{3,2,0,1:T(8,128)(2,1)S(1)}, u32[]{:S(2)}, u32[]{:S(2)}) %all-to-all-start.3) | async-done | bytes 368672 | tf_op jit(solution)/shard_map/all_to_all | solution.py:128
  338.5 5.2 %all-to-all-start.1 = ((bf16[1,16,9,1280]{3,2,0,1:T(8,128)(2,1)}), bf16[1,16,9,1280]{3,2,0,1:T(8,128)(2,1)S(1)}, u32[]{:S(2)}, u32[]{:S(2)}) async-start(bf16[1,16,9,1280]{3,2,0,1:T(8,128)(2,1)} %bitcast.31), calls=%async_computation.1 | async-start | bytes 1310720 | tf_op jit(solution)/shard_map/all_to_all | solution.py:129
  344.4 1.6 reshape.215
  346.0 18.3 %all-to-all-done.1 = bf16[1,16,9,1280]{3,2,0,1:T(8,128)(2,1)S(1)} async-done(((bf16[1,16,9,1280]{3,2,0,1:T(8,128)(2,1)}), bf16[1,16,9,1280]{3,2,0,1:T(8,128)(2,1)S(1)}, u32[]{:S(2)}, u32[]{:S(2)}) %all-to-all-start.1) | async-done | bytes 368672 | tf_op jit(solution)/shard_map/all_to_all | solution.py:129
  364.9 3.2 fusion.69
  368.1 1.9 fusion.20
  370.8 28.3 %all_to_all.55 = bf16[16,1,9,1280]{3,2,1,0:T(8,128)(2,1)S(1)} all-to-all(bf16[16,1,9,1280]{3,2,1,0:T(8,128)(2,1)S(1)} %reshape.216), channel_id=1, replica_groups=mesh['view'=16,'row'=16] {'view'}, dimensions={0} | all-to-all | bytes 737280 | tf_op jit(solution)/shard_map/all_to_all | solution.py:53
  399.4 3.3 fusion.12
  (81 shorter events, 11.3 us)
Async XLA Ops:
  6.5 65.9 %copy-start = (bf16[64,2560]{1,0:T(8,128)(2,1)S(1)}, bf16[64,2560]{1,0:T(8,128)(2,1)}, u32[]{:S(2)}) copy-start(bf16[64,2560]{1,0:T(8,128)(2,1)} %param.18) | copy-start | bytes 983044
  6.5 66.2 %copy-start.3 = (bf16[1,1,2,72,1280]{4,3,2,1,0:T(8,128)(2,1)S(1)}, bf16[1,1,2,72,1280]{4,3,2,1,0:T(8,128)(2,1)}, u32[]{:S(2)}) copy-start(bf16[1,1,2,72,1280]{4,3,2,1,0:T(8,128)(2,1)} %param.13) | copy-start | bytes 1105924
  6.5 66.2 %copy-start.6 = (f32[1280]{0:T(1024)S(1)}, f32[1280]{0:T(1024)}, u32[]{:S(2)}) copy-start(f32[1280]{0:T(1024)} %param.14) | copy-start | bytes 15364
  6.5 66.2 %copy-start.5 = (f32[1280]{0:T(1024)S(1)}, f32[1280]{0:T(1024)}, u32[]{:S(2)}) copy-start(f32[1280]{0:T(1024)} %param.15) | copy-start | bytes 15364
  6.5 111.6 %all-gather.4.cloned.1.call-start = ((), (), s32[]{:S(2)}) async-start(), calls=%async_computation.5 | async-start | bytes 6266880 | tf_op jit(solution)/shard_map/all_gather | solution.py:97
  73.8 209.3 %all-gather.6.cloned.1.call-start = ((), (), s32[]{:S(2)}) async-start(), calls=%async_computation.6 | async-start | bytes 10444800 | tf_op jit(solution)/shard_map/all_gather | solution.py:108
  74.6 324.8 %all-gather.8.cloned.1.call-start = ((), (), s32[]{:S(2)}) async-start(), calls=%async_computation.7 | async-start | bytes 3481600 | tf_op jit(solution)/shard_map/all_gather | solution.py:139
  75.3 78.3 %copy-start.4 = (bf16[3,3,1280,80]{2,3,1,0:T(8,128)(2,1)S(1)}, bf16[3,3,1280,80]{2,3,1,0:T(8,128)(2,1)}, u32[]{:S(2)}) copy-start(bf16[3,3,1280,80]{2,3,1,0:T(8,128)(2,1)} %param.20) | copy-start | bytes 5529604
  153.6 11.6 %slice-start.6 = ((s8[5898240]{0:T(1024)(128)(4,1)}), s8[4194304]{0:T(1024)(128)(4,1)S(1)}, s32[]{:S(2)}) async-start(s8[5898240]{0:T(1024)(128)(4,1)} %bitcast.127), calls=%async_computation.14 | async-start | bytes 8388608
  158.3 4.8 %copy-start.2 = (bf16[1,1,32,72,1280]{4,3,1,0,2:T(8,128)(2,1)S(1)}, bf16[1,1,32,72,1280]{4,3,1,0,2:T(8,128)(2,1)}, u32[]{:S(2)}) copy-start(bf16[1,1,32,72,1280]{4,3,1,0,2:T(8,128)(2,1)} %get-tuple-element.11) | copy-start | bytes 17694724
  158.4 6.8 %slice-start.7 = ((s8[5898240]{0:T(1024)(128)(4,1)}), s8[1703936]{0:T(1024)(128)(4,1)S(1)}, s32[]{:S(2)}) async-start(s8[5898240]{0:T(1024)(128)(4,1)} %bitcast.127), calls=%async_computation.15 | async-start | bytes 3407872
  163.2 3.9 slice-start
  163.2 6.0 %slice-start.4 = ((s8[5898240]{0:T(1024)(128)(4,1)}), s8[4194304]{0:T(1024)(128)(4,1)S(1)}, s32[]{:S(2)}) async-start(s8[5898240]{0:T(1024)(128)(4,1)} %bitcast.124), calls=%async_computation.12 | async-start | bytes 8388608
  165.1 2.2 slice-start.1
  165.2 4.1 slice-start.5
  167.3 3.9 slice-start.2
  169.2 2.2 slice-start.3
  178.2 24.8 %copy-start.7 = (f32[1280]{0:T(1024)S(1)}, f32[1280]{0:T(1024)}, u32[]{:S(2)}) copy-start(f32[1280]{0:T(1024)} %param.21) | copy-start | bytes 15364
  178.2 25.3 %copy-start.8 = (f32[1280]{0:T(1024)S(1)}, f32[1280]{0:T(1024)}, u32[]{:S(2)}) copy-start(f32[1280]{0:T(1024)} %param.22) | copy-start | bytes 15364
  287.2 26.5 %all-to-all-start.2 = ((bf16[1,16,9,1280]{3,2,0,1:T(8,128)(2,1)}), bf16[1,16,9,1280]{3,2,0,1:T(8,128)(2,1)S(1)}, u32[]{:S(2)}, u32[]{:S(2)}) async-start(bf16[1,16,9,1280]{3,2,0,1:T(8,128)(2,1)} %bitcast.33), calls=%async_computation.2 | async-start | bytes 1310720 | tf_op jit(solution)/shard_map/all_to_all | solution.py:127
  294.6 49.1 %copy-start.9 = (f32[20]{0:T(128)S(1)}, f32[20]{0:T(128)}, u32[]{:S(2)}) copy-start(f32[20]{0:T(128)} %param.25) | copy-start | bytes 244
  313.7 24.8 %all-to-all-start.3 = ((bf16[1,16,9,1280]{3,2,0,1:T(8,128)(2,1)}), bf16[1,16,9,1280]{3,2,0,1:T(8,128)(2,1)S(1)}, u32[]{:S(2)}, u32[]{:S(2)}) async-start(bf16[1,16,9,1280]{3,2,0,1:T(8,128)(2,1)} %bitcast.35), calls=%async_computation.3 | async-start | bytes 1310720 | tf_op jit(solution)/shard_map/all_to_all | solution.py:128
  338.5 25.8 %all-to-all-start.1 = ((bf16[1,16,9,1280]{3,2,0,1:T(8,128)(2,1)}), bf16[1,16,9,1280]{3,2,0,1:T(8,128)(2,1)S(1)}, u32[]{:S(2)}, u32[]{:S(2)}) async-start(bf16[1,16,9,1280]{3,2,0,1:T(8,128)(2,1)} %bitcast.31), calls=%async_computation.1 | async-start | bytes 1310720 | tf_op jit(solution)/shard_map/all_to_all | solution.py:129
  368.1 34.6 %copy-start.1 = (bf16[64,2560]{1,0:T(8,128)(2,1)S(1)}, bf16[64,2560]{1,0:T(8,128)(2,1)}, u32[]{:S(2)}) copy-start(bf16[64,2560]{1,0:T(8,128)(2,1)} %param.18) | copy-start | bytes 983044
Sparse Core Ops, SparseCore 0:
  73.9 44.1 all-gather.3
  120.7 162.3 all-gather.5
  285.7 106.9 all-gather.7
where the time goes:
time: 410 us; the launch traced here: 409 us
  waiting for transfers between devices  176 us (43%)
  blocking collectives  110 us (27%)
  matrix products  45.2 us (11%)
  local copies, waits for them, and re-layouts  44.5 us (11%)
  between operations  14.9 us (4%)
  starting transfers between devices  14.6 us (4%)
  other arithmetic  4.32 us (1%)
    all_gather x1, waiting for transfers between devices, local(): weights_in = lax.all_gather(attn_in, 'view', axis=2, tiled=True)  79.4 us
    all_gather x1, waiting for transfers between devices, local(): all_rows_act = lax.all_gather(activated, 'row', axis=2, tiled=True)  42.8 us
    slice x1, local copies, waits for them, and re-layouts, convolve(): padded[:, :, tap_row:tap_row + out_rows, tap_col:tap_col + out_cols, :]  35.5 us
    psum x1, blocking collectives, local(): summed = lax.psum(jnp.sum(grouped, axis=(2, 3, 5)), 'row')  29.7 us
    psum x1, blocking collectives, local(): spread = lax.psum(jnp.sum(centred * centred, axis=(2, 3, 5)), 'row')  28.6 us
    all_to_all x1, blocking collectives, send_back(): lax.all_to_all(mixed, 'view', split_axis=0, concat_axis=1, tiled=True)  28.3 us
    dot_general x9, matrix products, convolve(): jnp.dot(tap_rows, weight[tap_row, tap_col], preferred_element_type=jnp.fl...  23.9 us
    all_to_all x1, blocking collectives, local(): lax.all_to_all(partial_out, 'row', split_axis=2, concat_axis=4, tiled=True)  23.5 us
  transfers between devices with their start and end apart: 6, of which 5 were waited for; matrix products, arithmetic and copies ran while one was open for 20% of the time, Pallas kernels for 0%

commit v1 on v0

--- a/solution.py
+++ b/solution.py
@@ -9,22 +9,6 @@
 
 
 epsilon = 1e-05
-
-
-def convolve(padded, weight, out_rows, out_cols):
-    channels = padded.shape[-1]
-    summed = jnp.zeros(
-        (padded.shape[0] * padded.shape[1] * out_rows * out_cols, weight.shape[-1]), jnp.float32
-    )
-    for tap_row in range(3):
-        for tap_col in range(3):
-            tap_rows = padded[
-                :, :, tap_row : tap_row + out_rows, tap_col : tap_col + out_cols, :
-            ].reshape(-1, channels)
-            summed = summed + jnp.dot(
-                tap_rows, weight[tap_row, tap_col], preferred_element_type=jnp.float32
-            )
-    return summed.reshape(padded.shape[0], padded.shape[1], out_rows, out_cols, weight.shape[-1])
 
 
 def attend(query, key_block, value, head_scale):
@@ -70,16 +54,21 @@
 ):
     samples, local_views, local_rows, local_cols, channels = latent.shape
     width_out = ln_gain.shape[0]
-    x_float = latent.astype(jnp.float32)
+    out_part = conv_w.shape[-1]
+    row_devices = lax.axis_size("row")
+    whole = lax.all_gather(latent, "row", axis=2, tiled=True)
+    whole, attn_in, attn_out = lax.optimization_barrier((whole, attn_in, attn_out))
+    weights_in = lax.all_gather(attn_in, "view", axis=0, tiled=False)
+    weights_out = lax.all_gather(attn_out, "view", axis=0, tiled=True)
+
+    all_rows = whole.shape[2]
+    x_float = whole.astype(jnp.float32)
     grouped = x_float.reshape(
-        samples, local_views, local_rows, local_cols, GROUPS, channels // GROUPS
+        samples, local_views, all_rows, local_cols, GROUPS, channels // GROUPS
     )
-    entries = local_rows * local_cols * (channels // GROUPS) * lax.axis_size("row")
-    summed = lax.psum(jnp.sum(grouped, axis=(2, 3, 5)), "row")
-    average = (summed / entries)[:, :, None, None, :, None]
+    average = jnp.mean(grouped, axis=(2, 3, 5), keepdims=True)
     centred = grouped - average
-    spread = lax.psum(jnp.sum(centred * centred, axis=(2, 3, 5)), "row")
-    variance = (spread / entries)[:, :, None, None, :, None]
+    variance = jnp.mean(centred * centred, axis=(2, 3, 5), keepdims=True)
     normed = (centred * lax.rsqrt(variance + epsilon)).reshape(x_float.shape)
     cam_hot = (cam_idx[:, :, None] == jnp.arange(cam_table.shape[0], dtype=jnp.int32)).astype(
         jnp.bfloat16
@@ -94,18 +83,25 @@
     film_shift = film_rows[:, :, None, None, channels:]
     hidden = (normed * gn_gain + gn_bias) * (1.0 + film_scale) + film_shift
     activated = jax.nn.silu(hidden).astype(jnp.bfloat16)
-    all_rows_act = lax.all_gather(activated, "row", axis=2, tiled=True)
-    padded = jnp.pad(all_rows_act, ((0, 0), (0, 0), (1, 1), (1, 1), (0, 0)))
-    partial_out = convolve(padded, conv_w, all_rows_act.shape[2], local_cols)
-    conv_out = lax.all_to_all(partial_out, "row", split_axis=2, concat_axis=4, tiled=True)
-    resid_out = (x_float + conv_out + conv_bias).astype(jnp.bfloat16)
+    conv_out = lax.conv_general_dilated(
+        activated.reshape(samples * local_views, all_rows, local_cols, channels),
+        conv_w,
+        window_strides=(1, 1),
+        padding=((1, 1), (1, 1)),
+        dimension_numbers=("NHWC", "HWIO", "NHWC"),
+        preferred_element_type=jnp.float32,
+    ).reshape(samples, local_views, all_rows, local_cols, out_part)
+    me = lax.axis_index("row")
+    bias_part = lax.dynamic_slice_in_dim(conv_bias, me * out_part, out_part)
+    latent_part = lax.dynamic_slice_in_dim(whole, me * out_part, out_part, axis=4)
+    resid_part = (latent_part.astype(jnp.float32) + conv_out + bias_part).astype(jnp.bfloat16)
+    resid_out = lax.all_to_all(resid_part, "row", split_axis=2, concat_axis=4, tiled=True)
     resid_float = resid_out.astype(jnp.float32)
     middle = jnp.mean(resid_float, axis=-1, keepdims=True)
     spread_y = jnp.mean((resid_float - middle) ** 2, axis=-1, keepdims=True)
     normed_y = ((resid_float - middle) * lax.rsqrt(spread_y + epsilon) * ln_gain).astype(
         jnp.bfloat16
     )
-    weights_in = lax.all_gather(attn_in, "view", axis=2, tiled=True)
     view_devices = lax.axis_size("view")
     per_device = samples * local_rows * local_cols // view_devices
     pixel_major = jnp.moveaxis(normed_y, 1, 0).reshape(
@@ -116,7 +112,12 @@
         block_shape = pixel_block.shape
         flat_block = pixel_block.reshape(-1, width_out)
         return (
-            jnp.dot(flat_block, weights_in[matrix_index], preferred_element_type=jnp.float32)
+            jnp.einsum(
+                "pc,jcd->pjd",
+                flat_block,
+                weights_in[:, matrix_index],
+                preferred_element_type=jnp.float32,
+            )
             .astype(jnp.bfloat16)
             .reshape(block_shape)
         )
@@ -134,11 +135,7 @@
         mixed.reshape(local_views, samples, local_rows, local_cols, width_out), 0, 1
     )
     flat_mixed = mixed.reshape(-1, width_out)
-    projected = jnp.dot(
-        flat_mixed,
-        lax.all_gather(attn_out, "view", axis=0, tiled=True),
-        preferred_element_type=jnp.float32,
-    )
+    projected = jnp.dot(flat_mixed, weights_out, preferred_element_type=jnp.float32)
     return (resid_float + projected.reshape(resid_float.shape)).astype(jnp.bfloat16)
 
 

time: 410 us -> 345 us (0.84)
  blocking collectives: 110 us -> 0 us
  waiting for transfers between devices: 176 us -> 211 us
  other arithmetic: 4.32 us -> 19 us
  local copies, waits for them, and re-layouts: 44.5 us -> 31.3 us
  starting transfers between devices: 14.6 us -> 25.1 us
    psum x2 -> x0, blocking collectives: 58.3 us -> none  [the longest x1 29.7 us: local(): summed = lax.psum(jnp.sum(grouped, axis=(2, 3, 5)), 'row')]
    all_to_all x2 -> x0, blocking collectives: 51.8 us -> none  [the longest x1 28.3 us: send_back(): lax.all_to_all(mixed, 'view', split_axis=0, concat_axis=1, tiled=True)]
    slice x1 -> x0, local copies, waits for them, and re-layouts: 35.5 us -> none  [convolve(): padded[:, :, tap_row:tap_row + out_rows, tap_col:tap_col + out_cols, :]]
    all_to_all x0 -> x2, waiting for transfers between devices: none -> 30.7 us  [the longest x1 19.9 us: send_back(): lax.all_to_all(mixed, 'view', split_axis=0, concat_axis=1, tiled=True)]
    dot_general x13 -> x4, matrix products: 36.7 us -> 14.1 us  [the longest x3 10.6 us: project(): jnp.einsum('pc,jcd->pjd', flat_block, weights_in[:, matrix_index], prefer...]
    conv_general_dilated x0 -> x1, matrix products: none -> 18.1 us  [local(): lax.conv_general_dilated(activated.reshape(samples * local_views, all_row...]
    all_gather x3, waiting for transfers between devices: 122 us -> 132 us  [the longest x1 82.8 us: local(): weights_in = lax.all_gather(attn_in, 'view', axis=0, tiled=False)]
    all_to_all x0 -> x2, starting transfers between devices: none -> 9.7 us  [the longest x1 5.18 us: send_back(): lax.all_to_all(mixed, 'view', split_axis=0, concat_axis=1, tiled=True)]
  transfers between devices with their start and end apart: 6 -> 8, of which waited for: 5 -> 7; matrix products, arithmetic and copies ran while one was open for 20% -> 25% of each run, Pallas kernels for 0% -> 0%
where the time goes in v1:
time: 345 us; the launch traced here: 343 us
  waiting for transfers between devices  211 us (61%)
  matrix products  41.6 us (12%)
  local copies, waits for them, and re-layouts  31.3 us (9%)
  starting transfers between devices  25.1 us (7%)
  other arithmetic  19 us (6%)
  between operations  14.8 us (4%)
    all_gather x1, waiting for transfers between devices, local(): weights_in = lax.all_gather(attn_in, 'view', axis=0, tiled=False)  82.8 us
    all_gather x1, waiting for transfers between devices, local(): whole = lax.all_gather(latent, 'row', axis=2, tiled=True)  49.7 us
    all_to_all x1, waiting for transfers between devices, send_back(): lax.all_to_all(mixed, 'view', split_axis=0, concat_axis=1, tiled=True)  19.9 us
    conv_general_dilated x1, matrix products, local(): lax.conv_general_dilated(activated.reshape(samples * local_views, all_row...  18.1 us
    all_to_all x1, waiting for transfers between devices, local(): lax.all_to_all(triple_in[2], 'view', split_axis=1, concat_axis=0, tiled=T...  17.3 us
    all_to_all x1, waiting for transfers between devices, local(): lax.all_to_all(triple_in[0], 'view', split_axis=1, concat_axis=0, tiled=T...  17.3 us
    all_to_all x1, waiting for transfers between devices, local(): lax.all_to_all(triple_in[1], 'view', split_axis=1, concat_axis=0, tiled=T...  12.4 us
    all_to_all x1, waiting for transfers between devices, local(): lax.all_to_all(resid_part, 'row', split_axis=2, concat_axis=4, tiled=True)  10.8 us
  transfers between devices with their start and end apart: 8, of which 7 were waited for; matrix products, arithmetic and copies ran while one was open for 25% of the time, Pallas kernels for 0%

profile of v1, /device:TPU:1, one launch (start us, length us, event | category | flops | bytes accessed | tf_op | source)
XLA Modules:
  0.0 342.6 jit_solution(2853809703106247200)
XLA Ops:
  7.3 49.7 %all-gather.5.cloned.1.call-done = bf16[1,1,32,72,1280]{4,3,1,0,2:T(8,128)(2,1)} async-done(((bf16[1,1,2,72,1280]{4,3,1,0,2:T(8,128)(2,1)}), bf16[1,1,32,72,1280]{4,3,1,0,2:T(8,128)(2,1)}) %all-gather.5.cloned.1.call-update) | async-done | bytes 5898256 | tf_op jit(solution)/shard_map/all_gather | solution.py:59
  59.5 3.2 convolution_reduce_fusion
  63.6 6.7 %copy.63 = bf16[1,1,32,72,1280]{4,2,3,1,0:T(8,128)(2,1)} copy(bf16[1,1,32,72,1280]{4,3,1,0,2:T(8,128)(2,1)} %all-gather.5.cloned.1.call-done) | data formatting | bytes 11796480 | tf_op jit(solution)/shard_map/optimization_barrier | solution.py:60
  71.6 4.9 %fusion.4 = f32[1280]{0:T(1024)S(1)} fusion(f32[1280]{0:T(1024)S(1)} %sub.47, bf16[1,1,32,72,1280]{4,3,1,0,2:T(8,128)(2,1)} %all-gather.5.cloned.1.call-done), kind=kLoop, calls=%fused_computation.7 | loop fusion | flops 11795200 | bytes 5908480 | tf_op jit(solution)/shard_map/reduce_sum | solution.py:71
  76.9 8.1 %fusion.16 = bf16[32,1,72,1280]{3,0,2,1:T(8,128)(2,1)S(1)} fusion(f32[1280]{0:T(1024)S(1)} %get-tuple-element.12, f32[1280]{0:T(1024)S(1)} %get-tuple-element.11, f32[1280]{0:T(1024)S(1)} %copy-done.5, f32[1280]{0:T(1024)S(1)} %copy-done.6, f32[1280]{0:T(1024)S(1)} %mul.93, f32[1280]{0:T(1024)S(1)} %sub.47, ...), kind=kLoop, calls=%fused_computation.19 | loop fusion | flops 35389440 | bytes 11827200 | tf_op jit(solution)/shard_map/reshape | solution.py:87
  85.8 3.6 %copy.66 = bf16[32,1,8,10,1280]{4,2,3,0,1:T(8,128)(2,1)S(1)} copy(bf16[32,1,8,10,1280]{4,0,3,2,1:T(8,128)(2,1)S(1)} %bitcast.94) | data formatting | bytes 13107200 | tf_op jit(solution)/shard_map/conv_general_dilated | solution.py:86
  89.5 2.7 copy-done.2
  92.5 18.1 %fusion.34 = f32[32,8,10,80]{3,1,2,0:T(8,128)S(1)} fusion(bf16[3,3,1280,80]{2,3,1,0:T(8,128)(2,1)S(1)} %copy-done, bf16[32,1,7,2,1280]{4,2,3,0,1:T(8,128)(2,1)S(1)} %slice.24, bf16[32,1,8,10,1280]{4,2,3,0,1:T(8,128)(2,1)} %copy-done.2, pred[8,10]{0,1:T(8,128)(4,1)S(1)} %copy-done.8), kind=kOutput, calls=%fused_computation.37 | convolution fusion | flops 4644085760 | bytes 10362960 | tf_op jit(solution)/shard_map/conv_general_dilated | solution.py:86
  111.1 1.6 fusion.43
  113.8 4.5 %all-to-all-start = ((bf16[1,1,32,72,80]{4,3,1,0,2:T(8,128)(2,1)}), bf16[1,1,32,72,80]{4,3,1,0,2:T(8,128)(2,1)S(1)}, u32[]{:S(2)}, u32[]{:S(2)}) async-start(bf16[1,1,32,72,80]{4,3,1,0,2:T(8,128)(2,1)} %copy.68), calls=%async_computation | async-start | bytes 1179648 | tf_op jit(solution)/shard_map/all_to_all | solution.py:98
  118.4 10.8 %all-to-all-done = bf16[1,1,32,72,80]{4,3,1,0,2:T(8,128)(2,1)S(1)} async-done(((bf16[1,1,32,72,80]{4,3,1,0,2:T(8,128)(2,1)}), bf16[1,1,32,72,80]{4,3,1,0,2:T(8,128)(2,1)S(1)}, u32[]{:S(2)}, u32[]{:S(2)}) %all-to-all-start) | async-done | bytes 368672 | tf_op jit(solution)/shard_map/all_to_all | solution.py:98
  130.0 2.0 multiply_reduce_fusion
  133.0 82.8 %all-gather.9.cloned.1.call-done = bf16[48,1280,80]{1,2,0:T(8,128)(2,1)} async-done(((bf16[3,1280,80]{1,2,0:T(8,128)(2,1)}), bf16[48,1280,80]{1,2,0:T(8,128)(2,1)}) %all-gather.9.cloned.1.call-update) | async-done | bytes 9830416 | tf_op jit(solution)/shard_map/all_gather | solution.py:61
  215.8 3.5 %fusion.38 = bf16[144,16,80]{2,0,1:T(8,128)(2,1)S(1)} fusion(bf16[144,1280,1]{1,0,2:T(8,128)(2,1)S(1)} %reshape.277, bf16[16,3,1280,80]{2,3,1,0:T(8,128)(2,1)} %bitcast.100), kind=kOutput, calls=%fused_computation.39 | convolution fusion | flops 472043520 | bytes 4014080 | tf_op jit(solution)/shard_map/pc,jcd->pjd/dot_general | solution.py:115
  219.5 1.7 reshape.250
  221.1 4.2 %all-to-all-start.2 = ((bf16[1,16,9,1280]{3,2,0,1:T(8,128)(2,1)}), bf16[1,16,9,1280]{3,2,0,1:T(8,128)(2,1)S(1)}, u32[]{:S(2)}, u32[]{:S(2)}) async-start(bf16[1,16,9,1280]{3,2,0,1:T(8,128)(2,1)} %bitcast.15), calls=%async_computation.2 | async-start | bytes 1310720 | tf_op jit(solution)/shard_map/all_to_all | solution.py:128
  225.3 3.5 %fusion.39 = bf16[144,16,80]{2,0,1:T(8,128)(2,1)S(1)} fusion(bf16[144,1280,1]{1,0,2:T(8,128)(2,1)S(1)} %reshape.277, bf16[16,3,1280,80]{2,3,1,0:T(8,128)(2,1)} %bitcast.101), kind=kOutput, calls=%fused_computation.40 | convolution fusion | flops 472043520 | bytes 4014080 | tf_op jit(solution)/shard_map/pc,jcd->pjd/dot_general | solution.py:115
  229.0 1.7 reshape.252
  230.7 17.3 %all-to-all-done.2 = bf16[1,16,9,1280]{3,2,0,1:T(8,128)(2,1)S(1)} async-done(((bf16[1,16,9,1280]{3,2,0,1:T(8,128)(2,1)}), bf16[1,16,9,1280]{3,2,0,1:T(8,128)(2,1)S(1)}, u32[]{:S(2)}, u32[]{:S(2)}) %all-to-all-start.2) | async-done | bytes 368672 | tf_op jit(solution)/shard_map/all_to_all | solution.py:128
  248.0 5.4 %all-to-all-start.3 = ((bf16[1,16,9,1280]{3,2,0,1:T(8,128)(2,1)}), bf16[1,16,9,1280]{3,2,0,1:T(8,128)(2,1)S(1)}, u32[]{:S(2)}, u32[]{:S(2)}) async-start(bf16[1,16,9,1280]{3,2,0,1:T(8,128)(2,1)} %bitcast.17), calls=%async_computation.3 | async-start | bytes 1310720 | tf_op jit(solution)/shard_map/all_to_all | solution.py:129
  253.4 3.5 %fusion.37 = bf16[144,16,80]{2,0,1:T(8,128)(2,1)S(1)} fusion(bf16[144,1280,1]{1,0,2:T(8,128)(2,1)S(1)} %reshape.277, bf16[16,3,1280,80]{2,3,1,0:T(8,128)(2,1)} %bitcast.102), kind=kOutput, calls=%fused_computation.38 | convolution fusion | flops 472043520 | bytes 4014080 | tf_op jit(solution)/shard_map/pc,jcd->pjd/dot_general | solution.py:115
  257.1 1.7 reshape.248
  258.8 12.4 %all-to-all-done.3 = bf16[1,16,9,1280]{3,2,0,1:T(8,128)(2,1)S(1)} async-done(((bf16[1,16,9,1280]{3,2,0,1:T(8,128)(2,1)}), bf16[1,16,9,1280]{3,2,0,1:T(8,128)(2,1)S(1)}, u32[]{:S(2)}, u32[]{:S(2)}) %all-to-all-start.3) | async-done | bytes 368672 | tf_op jit(solution)/shard_map/all_to_all | solution.py:129
  271.1 5.7 %all-to-all-start.1 = ((bf16[1,16,9,1280]{3,2,0,1:T(8,128)(2,1)}), bf16[1,16,9,1280]{3,2,0,1:T(8,128)(2,1)S(1)}, u32[]{:S(2)}, u32[]{:S(2)}) async-start(bf16[1,16,9,1280]{3,2,0,1:T(8,128)(2,1)} %bitcast.13), calls=%async_computation.1 | async-start | bytes 1310720 | tf_op jit(solution)/shard_map/all_to_all | solution.py:130
  276.9 1.6 reshape.281
  279.1 17.3 %all-to-all-done.1 = bf16[1,16,9,1280]{3,2,0,1:T(8,128)(2,1)S(1)} async-done(((bf16[1,16,9,1280]{3,2,0,1:T(8,128)(2,1)}), bf16[1,16,9,1280]{3,2,0,1:T(8,128)(2,1)S(1)}, u32[]{:S(2)}, u32[]{:S(2)}) %all-to-all-start.1) | async-done | bytes 368672 | tf_op jit(solution)/shard_map/all_to_all | solution.py:130
  296.4 1.6 reshape.280
  298.0 3.3 fusion.61
  301.2 1.8 fusion.40
  304.7 5.2 %all-to-all-start.4 = ((bf16[16,1,9,1280]{3,2,1,0:T(8,128)(2,1)}), bf16[16,1,9,1280]{3,2,1,0:T(8,128)(2,1)}, u32[]{:S(2)}, u32[]{:S(2)}) async-start(bf16[16,1,9,1280]{3,2,1,0:T(8,128)(2,1)} %reshape.283), calls=%async_computation.4 | async-start | bytes 1310720 | tf_op jit(solution)/shard_map/all_to_all | solution.py:37
  311.4 19.9 %all-to-all-done.4 = bf16[16,1,9,1280]{3,2,1,0:T(8,128)(2,1)} async-done(((bf16[16,1,9,1280]{3,2,1,0:T(8,128)(2,1)}), bf16[16,1,9,1280]{3,2,1,0:T(8,128)(2,1)}, u32[]{:S(2)}, u32[]{:S(2)}) %all-to-all-start.4) | async-done | bytes 368672 | tf_op jit(solution)/shard_map/all_to_all | solution.py:37
  332.6 3.5 %fusion.29 = bf16[1,1,2,72,1280]{4,3,2,1,0:T(8,128)(2,1)} fusion(f32[2,72,1280]{2,1,0:T(8,128)} %reshape.262, bf16[2,72,1280]{2,1,0:T(8,128)(2,1)S(1)} %dot_general.33, bf16[1280,1280]{1,0:T(8,128)(2,1)} %all-gather.7.cloned.1.call-done), kind=kOutput, calls=%fused_computation.31 | convolution fusion | flops 472227840 | bytes 4751360 | tf_op jit(solution)/shard_map/dot_general | solution.py:138
  (68 shorter events, 14.5 us)
Async XLA Ops:
  6.5 86.0 %copy-start = (bf16[3,3,1280,80]{2,3,1,0:T(8,128)(2,1)S(1)}, bf16[3,3,1280,80]{2,3,1,0:T(8,128)(2,1)}, u32[]{:S(2)}) copy-start(bf16[3,3,1280,80]{2,3,1,0:T(8,128)(2,1)} %param.20) | copy-start | bytes 5529604
  6.5 50.4 %all-gather.5.cloned.1.call-start = ((), (), s32[]{:S(2)}) async-start(), calls=%async_computation.5 | async-start | bytes 6266880 | tf_op jit(solution)/shard_map/all_gather | solution.py:59
  7.3 208.5 %all-gather.9.cloned.1.call-start = ((), (), s32[]{:S(2)}) async-start(), calls=%async_computation.7 | async-start | bytes 10444800 | tf_op jit(solution)/shard_map/all_gather | solution.py:61
  57.0 275.6 %all-gather.7.cloned.1.call-start = ((), (), s32[]{:S(2)}) async-start(), calls=%async_computation.6 | async-start | bytes 3481600 | tf_op jit(solution)/shard_map/all_gather | solution.py:62
  63.6 6.7 %slice-start = ((s8[5898240]{0:T(1024)(128)(4,1)}), s8[4194304]{0:T(1024)(128)(4,1)S(1)}, s32[]{:S(2)}) async-start(s8[5898240]{0:T(1024)(128)(4,1)} %bitcast.92), calls=%async_computation.8 | async-start | bytes 8388608
  63.6 6.7 %slice-start.1 = ((s8[5898240]{0:T(1024)(128)(4,1)}), s8[1703936]{0:T(1024)(128)(4,1)S(1)}, s32[]{:S(2)}) async-start(s8[5898240]{0:T(1024)(128)(4,1)} %bitcast.92), calls=%async_computation.9 | async-start | bytes 3407872
  71.2 5.7 %copy-start.5 = (f32[1280]{0:T(1024)S(1)}, f32[1280]{0:T(1024)}, u32[]{:S(2)}) copy-start(f32[1280]{0:T(1024)} %param.15) | copy-start | bytes 15364
  71.2 5.7 %copy-start.6 = (f32[1280]{0:T(1024)S(1)}, f32[1280]{0:T(1024)}, u32[]{:S(2)}) copy-start(f32[1280]{0:T(1024)} %param.14) | copy-start | bytes 15364
  85.8 6.7 %copy-start.8 = (pred[8,10]{0,1:T(8,128)(4,1)S(1)}, pred[8,10]{0,1:T(8,128)(4,1)}, u32[]{:S(2)}) copy-start(pred[8,10]{0,1:T(8,128)(4,1)} %constant.38) | copy-start | bytes 244
  89.5 2.7 copy-start.2
  110.7 7.6 %copy-start.4 = (f32[1280]{0:T(1024)S(1)}, f32[1280]{0:T(1024)}, u32[]{:S(2)}) copy-start(f32[1280]{0:T(1024)} %param.22) | copy-start | bytes 15364
  113.8 15.4 %all-to-all-start = ((bf16[1,1,32,72,80]{4,3,1,0,2:T(8,128)(2,1)}), bf16[1,1,32,72,80]{4,3,1,0,2:T(8,128)(2,1)S(1)}, u32[]{:S(2)}, u32[]{:S(2)}) async-start(bf16[1,1,32,72,80]{4,3,1,0,2:T(8,128)(2,1)} %copy.68), calls=%async_computation | async-start | bytes 1179648 | tf_op jit(solution)/shard_map/all_to_all | solution.py:98
  221.1 26.8 %all-to-all-start.2 = ((bf16[1,16,9,1280]{3,2,0,1:T(8,128)(2,1)}), bf16[1,16,9,1280]{3,2,0,1:T(8,128)(2,1)S(1)}, u32[]{:S(2)}, u32[]{:S(2)}) async-start(bf16[1,16,9,1280]{3,2,0,1:T(8,128)(2,1)} %bitcast.15), calls=%async_computation.2 | async-start | bytes 1310720 | tf_op jit(solution)/shard_map/all_to_all | solution.py:128
  248.0 23.2 %all-to-all-start.3 = ((bf16[1,16,9,1280]{3,2,0,1:T(8,128)(2,1)}), bf16[1,16,9,1280]{3,2,0,1:T(8,128)(2,1)S(1)}, u32[]{:S(2)}, u32[]{:S(2)}) async-start(bf16[1,16,9,1280]{3,2,0,1:T(8,128)(2,1)} %bitcast.17), calls=%async_computation.3 | async-start | bytes 1310720 | tf_op jit(solution)/shard_map/all_to_all | solution.py:129
  253.4 23.4 %copy-start.7 = (f32[20]{0:T(128)S(1)}, f32[20]{0:T(128)}, u32[]{:S(2)}) copy-start(f32[20]{0:T(128)} %param.25) | copy-start | bytes 244
  271.1 25.3 %all-to-all-start.1 = ((bf16[1,16,9,1280]{3,2,0,1:T(8,128)(2,1)}), bf16[1,16,9,1280]{3,2,0,1:T(8,128)(2,1)S(1)}, u32[]{:S(2)}, u32[]{:S(2)}) async-start(bf16[1,16,9,1280]{3,2,0,1:T(8,128)(2,1)} %bitcast.13), calls=%async_computation.1 | async-start | bytes 1310720 | tf_op jit(solution)/shard_map/all_to_all | solution.py:130
  298.0 3.3 copy-start.3
  304.7 26.6 %all-to-all-start.4 = ((bf16[16,1,9,1280]{3,2,1,0:T(8,128)(2,1)}), bf16[16,1,9,1280]{3,2,1,0:T(8,128)(2,1)}, u32[]{:S(2)}, u32[]{:S(2)}) async-start(bf16[16,1,9,1280]{3,2,1,0:T(8,128)(2,1)} %reshape.283), calls=%async_computation.4 | async-start | bytes 1310720 | tf_op jit(solution)/shard_map/all_to_all | solution.py:37
  310.0 26.0 %copy-start.1 = (bf16[3,3,1280,80]{2,3,1,0:T(8,128)(2,1)S(1)}, bf16[3,3,1280,80]{2,3,1,0:T(8,128)(2,1)}, u32[]{:S(2)}) copy-start(bf16[3,3,1280,80]{2,3,1,0:T(8,128)(2,1)} %param.20) | copy-start | bytes 5529604
Sparse Core Ops, SparseCore 0:
  9.2 47.7 all-gather.4
  59.6 156.1 all-gather.8
  218.4 105.0 all-gather.6

commit v2 on v1

--- a/solution.py
+++ b/solution.py
@@ -55,11 +55,14 @@
     samples, local_views, local_rows, local_cols, channels = latent.shape
     width_out = ln_gain.shape[0]
     out_part = conv_w.shape[-1]
-    row_devices = lax.axis_size("row")
-    whole = lax.all_gather(latent, "row", axis=2, tiled=True)
+    whole = lax.all_gather(latent, ROW, axis=2, tiled=True)
     whole, attn_in, attn_out = lax.optimization_barrier((whole, attn_in, attn_out))
-    weights_in = lax.all_gather(attn_in, "view", axis=0, tiled=False)
-    weights_out = lax.all_gather(attn_out, "view", axis=0, tiled=True)
+    core = lax.axis_index("core")
+    half_in = attn_in.shape[1] // 2
+    half_out = attn_out.shape[1] // 2
+    in_half = lax.dynamic_slice_in_dim(attn_in, core * half_in, half_in, axis=1)
+    in_half = lax.all_gather(in_half, "view", axis=0, tiled=False)
+    out_half = lax.dynamic_slice_in_dim(attn_out, core * half_out, half_out, axis=1)
 
     all_rows = whole.shape[2]
     x_float = whole.astype(jnp.float32)
@@ -91,11 +94,13 @@
         dimension_numbers=("NHWC", "HWIO", "NHWC"),
         preferred_element_type=jnp.float32,
     ).reshape(samples, local_views, all_rows, local_cols, out_part)
-    me = lax.axis_index("row")
+    me = lax.axis_index("chip") * lax.axis_size("core") + core
     bias_part = lax.dynamic_slice_in_dim(conv_bias, me * out_part, out_part)
     latent_part = lax.dynamic_slice_in_dim(whole, me * out_part, out_part, axis=4)
     resid_part = (latent_part.astype(jnp.float32) + conv_out + bias_part).astype(jnp.bfloat16)
-    resid_out = lax.all_to_all(resid_part, "row", split_axis=2, concat_axis=4, tiled=True)
+    in_half, resid_part = lax.optimization_barrier((in_half, resid_part))
+    weights_in = lax.all_gather(in_half, "core", axis=0, tiled=False)
+    resid_out = lax.all_to_all(resid_part, ROW, split_axis=2, concat_axis=4, tiled=True)
     resid_float = resid_out.astype(jnp.float32)
     middle = jnp.mean(resid_float, axis=-1, keepdims=True)
     spread_y = jnp.mean((resid_float - middle) ** 2, axis=-1, keepdims=True)
@@ -108,47 +113,45 @@
         local_views, view_devices, per_device, width_out
     )
 
-    def project(pixel_block, matrix_index):
-        block_shape = pixel_block.shape
-        flat_block = pixel_block.reshape(-1, width_out)
-        return (
-            jnp.einsum(
-                "pc,jcd->pjd",
-                flat_block,
-                weights_in[:, matrix_index],
-                preferred_element_type=jnp.float32,
-            )
-            .astype(jnp.bfloat16)
-            .reshape(block_shape)
-        )
-
-    triple_in = (project(pixel_major, 0), project(pixel_major, 1), project(pixel_major, 2))
-    mixed = send_back(
-        attend(
-            lax.all_to_all(triple_in[0], "view", split_axis=1, concat_axis=0, tiled=True),
-            lax.all_to_all(triple_in[1], "view", split_axis=1, concat_axis=0, tiled=True),
-            lax.all_to_all(triple_in[2], "view", split_axis=1, concat_axis=0, tiled=True),
-            head_scale,
-        )
-    )
+    flat_block = pixel_major.reshape(-1, 2, width_out // 2)
+    triple_in = jnp.einsum(
+        "pkc,kjmcd->mpjd", flat_block, weights_in, preferred_element_type=jnp.float32
+    ).astype(jnp.bfloat16)
+    triple_in = triple_in.reshape((3,) + pixel_major.shape)
+    out_half, triple_in = lax.optimization_barrier((out_half, triple_in))
+    out_half = lax.all_gather(out_half, "view", axis=0, tiled=True)
+    triple_in = lax.all_to_all(triple_in, "view", split_axis=2, concat_axis=1, tiled=True)
+    mixed = send_back(attend(triple_in[0], triple_in[1], triple_in[2], head_scale))
+    out_half, mixed = lax.optimization_barrier((out_half, mixed))
+    weights_out = lax.all_gather(out_half, "core", axis=0, tiled=False)
     mixed = jnp.moveaxis(
         mixed.reshape(local_views, samples, local_rows, local_cols, width_out), 0, 1
     )
     flat_mixed = mixed.reshape(-1, width_out)
-    projected = jnp.dot(flat_mixed, weights_out, preferred_element_type=jnp.float32)
+    projected = jnp.einsum(
+        "pc,kcd->pkd", flat_mixed, weights_out, preferred_element_type=jnp.float32
+    )
     return (resid_float + projected.reshape(resid_float.shape)).astype(jnp.bfloat16)
 
 
+ROW = ("chip", "core")
+
+
 def solution(mesh):
+    cores = 2
+    split = jax.sharding.Mesh(
+        mesh.devices.reshape(mesh.shape["view"], mesh.shape["row"] // cores, cores),
+        ("view", "chip", "core"),
+    )
     placed = (
-        P(None, "view", "row", None, None),
+        P(None, "view", ROW, None, None),
         P(),
         P(),
         P(None, "view"),
         P(),
         P(),
         P(),
-        P(None, None, None, "row"),
+        P(None, None, None, ROW),
         P(),
         P(),
         P(None, None, "view"),
@@ -157,8 +160,8 @@
     )
     return jax.shard_map(
         local,
-        mesh=mesh,
+        mesh=split,
         in_specs=placed,
-        out_specs=P(None, "view", "row", None, None),
+        out_specs=P(None, "view", ROW, None, None),
         check_vma=False,
     )

time: 345 us -> 357 us (1.035); the launches traced: 343 us -> 350 us
  blocking collectives: 0 us -> 29.5 us
  waiting for transfers between devices: 211 us -> 184 us
  local copies, waits for them, and re-layouts: 31.3 us -> 45.9 us
  starting transfers between devices: 25.1 us -> 17.3 us
    all_to_all x5 -> x2, waiting for transfers between devices: 77.7 us -> 45.9 us  [the longest x1 36.5 us: local(): lax.all_to_all(triple_in, 'view', split_axis=2, concat_axis=1, tiled=True)]
    all_to_all x0 -> x1, blocking collectives: none -> 29.5 us  [send_back(): lax.all_to_all(mixed, 'view', split_axis=0, concat_axis=1, tiled=True)]
    all_to_all x5 -> x2, starting transfers between devices: 25 us -> 17.1 us  [the longest x1 9.02 us: local(): lax.all_to_all(triple_in, 'view', split_axis=2, concat_axis=1, tiled=True)]
    slice x0 -> x1, local copies, waits for them, and re-layouts: none -> 6.28 us  [local(): triple_in[2]]
    another operation x0 -> x3, local copies, waits for them, and re-layouts: none -> 5.82 us  [the longest x1 2.5 us: attend(): key_heads = key_block.reshape(view_count, item_count, head_count, head_size)]
    all_gather x0 -> x1, local copies, waits for them, and re-layouts: none -> 5.72 us  [local(): weights_out = lax.all_gather(out_half, 'core', axis=0, tiled=False)]
    all_gather x3 -> x5, waiting for transfers between devices: 132 us -> 137 us  [the longest x1 49.7 us: local(): whole = lax.all_gather(latent, ROW, axis=2, tiled=True)]
    reshape x6 -> x1, local copies, waits for them, and re-layouts: 8.78 us -> 5.65 us  [local(): triple_in = triple_in.reshape((3,) + pixel_major.shape)]
  transfers between devices with their start and end apart: 8 -> 7, of which waited for: 7 -> 7; matrix products, arithmetic and copies ran while one was open for 25% -> 22% of each run, Pallas kernels for 0% -> 0%
where the time goes in v2:
time: 357 us; the launch traced here: 350 us
  waiting for transfers between devices  184 us (52%)
  local copies, waits for them, and re-layouts  45.9 us (13%)
  matrix products  38.9 us (11%)
  blocking collectives  29.5 us (8%)
  other arithmetic  19.7 us (6%)
  starting transfers between devices  17.3 us (5%)
  between operations  15 us (4%)
    all_gather x1, waiting for transfers between devices, local(): whole = lax.all_gather(latent, ROW, axis=2, tiled=True)  49.7 us
    all_gather x1, waiting for transfers between devices, local(): in_half = lax.all_gather(in_half, 'view', axis=0, tiled=False)  49 us
    all_to_all x1, waiting for transfers between devices, local(): lax.all_to_all(triple_in, 'view', split_axis=2, concat_axis=1, tiled=True)  36.5 us
    all_to_all x1, blocking collectives, send_back(): lax.all_to_all(mixed, 'view', split_axis=0, concat_axis=1, tiled=True)  29.5 us
    all_gather x1, waiting for transfers between devices, local(): weights_out = lax.all_gather(out_half, 'core', axis=0, tiled=False)  20.9 us
    conv_general_dilated x1, matrix products, local(): lax.conv_general_dilated(activated.reshape(samples * local_views, all_row...  17 us
    all_gather x1, waiting for transfers between devices, local(): out_half = lax.all_gather(out_half, 'view', axis=0, tiled=True)  10.7 us
    all_to_all x1, waiting for transfers between devices, local(): lax.all_to_all(resid_part, ROW, split_axis=2, concat_axis=4, tiled=True)  9.36 us
  transfers between devices with their start and end apart: 7, of which 7 were waited for; matrix products, arithmetic and copies ran while one was open for 22% of the time, Pallas kernels for 0%

profile of v2, /device:TPU:1, one launch (start us, length us, event | category | flops | bytes accessed | tf_op | source)
XLA Modules:
  0.0 349.9 jit_solution(10321813126953900763)
XLA Ops:
  7.3 49.7 %all-gather.9.cloned.1.call-done = bf16[1,1,32,72,1280]{4,3,1,0,2:T(8,128)(2,1)} async-done(((bf16[1,1,2,72,1280]{4,3,1,0,2:T(8,128)(2,1)}), bf16[1,1,32,72,1280]{4,3,1,0,2:T(8,128)(2,1)}) %all-gather.9.cloned.1.call-update) | async-done | bytes 5898256 | tf_op jit(solution)/shard_map/all_gather | solution.py:58
  57.0 1.7 constant_dynamic-slice_fusion.1
  61.2 3.4 convolution_reduce_fusion
  65.2 1.3 dynamic_slice.14
  66.5 1.3 fusion.43
  67.9 6.8 %copy.79 = bf16[1,1,32,72,1280]{4,2,3,1,0:T(8,128)(2,1)} copy(bf16[1,1,32,72,1280]{4,3,1,0,2:T(8,128)(2,1)} %all-gather.9.cloned.1.call-done) | data formatting | bytes 11796480 | tf_op jit(solution)/shard_map/optimization_barrier | solution.py:59
  75.9 4.5 %fusion.4 = f32[1280]{0:T(1024)S(1)} fusion(f32[1280]{0:T(1024)S(1)} %sub.48, bf16[1,1,32,72,1280]{4,3,1,0,2:T(8,128)(2,1)} %all-gather.9.cloned.1.call-done), kind=kLoop, calls=%fused_computation.7 | loop fusion | flops 11795200 | bytes 5908480 | tf_op jit(solution)/shard_map/reduce_sum | solution.py:74
  80.8 8.3 %fusion.16 = bf16[32,1,72,1280]{3,0,2,1:T(8,128)(2,1)S(1)} fusion(f32[1280]{0:T(1024)S(1)} %copy-done.4, f32[1280]{0:T(1024)S(1)} %copy-done.3, f32[1280]{0:T(1024)S(1)} %copy-done.6, f32[1280]{0:T(1024)S(1)} %copy-done.7, f32[1280]{0:T(1024)S(1)} %mul.96, f32[1280]{0:T(1024)S(1)} %sub.48, bf16[1,1,32,72,1280]{4,3,1,0,2:T(8,128)(2,1)} %all-gather.9.cloned.1.call-done), kind=kLoop, calls=%fused_computation.19 | loop fusion | flops 35389440 | bytes 11827200 | tf_op jit(solution)/shard_map/reshape | solution.py:90
  89.9 3.6 %copy.82 = bf16[32,1,8,10,1280]{4,2,3,0,1:T(8,128)(2,1)S(1)} copy(bf16[32,1,8,10,1280]{4,0,3,2,1:T(8,128)(2,1)S(1)} %bitcast.78) | data formatting | bytes 13107200 | tf_op jit(solution)/shard_map/conv_general_dilated | solution.py:89
  93.9 17.0 %fusion.23 = f32[32,8,10,80]{3,1,2,0:T(8,128)S(1)} fusion(bf16[3,3,1280,80]{2,3,1,0:T(8,128)(2,1)S(1)} %copy-done, bf16[32,1,7,2,1280]{4,2,3,0,1:T(8,128)(2,1)S(1)} %slice.28, bf16[32,1,8,10,1280]{4,2,3,0,1:T(8,128)(2,1)S(1)} %copy.82, pred[8,10]{0,1:T(8,128)(4,1)S(1)} %copy-done.10), kind=kOutput, calls=%fused_computation.31 | convolution fusion | flops 4644085760 | bytes 10362960 | tf_op jit(solution)/shard_map/conv_general_dilated | solution.py:89
  111.4 1.7 fusion.29
  113.1 49.0 %all-gather.13.cloned.1.call-done = bf16[48,640,80]{1,2,0:T(8,128)(2,1)} async-done(((bf16[3,640,80]{1,2,0:T(8,128)(2,1)}), bf16[48,640,80]{1,2,0:T(8,128)(2,1)}) %all-gather.13.cloned.1.call-update) | async-done | bytes 4915216 | tf_op jit(solution)/shard_map/all_gather | solution.py:64
  163.2 8.1 %all-to-all-start = ((bf16[1,1,32,72,80]{4,3,1,0,2:T(8,128)(2,1)}), bf16[1,1,32,72,80]{4,3,1,0,2:T(8,128)(2,1)S(1)}, u32[]{:S(2)}, u32[]{:S(2)}) async-start(bf16[1,1,32,72,80]{4,3,1,0,2:T(8,128)(2,1)} %copy.84), calls=%async_computation | async-start | bytes 1179648 | tf_op jit(solution)/shard_map/all_to_all | solution.py:103
  172.0 9.4 %all-to-all-done = bf16[1,1,32,72,80]{4,3,1,0,2:T(8,128)(2,1)S(1)} async-done(((bf16[1,1,32,72,80]{4,3,1,0,2:T(8,128)(2,1)}), bf16[1,1,32,72,80]{4,3,1,0,2:T(8,128)(2,1)S(1)}, u32[]{:S(2)}, u32[]{:S(2)}) %all-to-all-start) | async-done | bytes 368672 | tf_op jit(solution)/shard_map/all_to_all | solution.py:103
  182.4 2.0 multiply_reduce_fusion
  185.5 6.3 %all-gather.15.cloned.1.call-done = bf16[32,3,640,80]{2,3,1,0:T(8,128)(2,1)} async-done(((bf16[16,3,640,80]{2,3,1,0:T(8,128)(2,1)}), bf16[32,3,640,80]{2,3,1,0:T(8,128)(2,1)}) %all-gather.15.cloned.1.call-update) | async-done | bytes 9830416 | tf_op jit(solution)/shard_map/all_gather | solution.py:102
  191.8 8.2 %fusion.38 = bf16[16,3,80,144,1]{2,3,1,0,4:T(8,128)(2,1)S(1)} fusion(bf16[2,16,3,640,80]{3,4,2,1,0:T(8,128)(2,1)} %bitcast.91, f32[144,2,640]{2,1,0:T(2,128)S(1)} %reshape.199, f32[2,640]{1,0:T(2,128)S(1)} %mul.106, f32[144]{0:T(256)S(1)} %rsqrt.21, f32[144]{0:T(256)S(1)} %div.35), kind=kOutput, calls=%fused_computation.53 | convolution fusion | flops 1416314880 | bytes 11679872 | tf_op jit(solution)/shard_map/pkc,kjmcd->mpjd/dot_general | solution.py:117
  200.1 1.7 copy.88
  201.8 5.7 %reshape.189 = bf16[3,1,16,9,1280]{4,0,3,2,1:T(4,128)(2,1)} reshape(bf16[3,144,16,80]{3,2,0,1:T(8,128)(2,1)} %copy.88) | data formatting | bytes 2211840 | tf_op jit(solution)/shard_map/reshape | solution.py:120
  207.5 9.0 %all-to-all-start.1 = ((bf16[3,1,16,9,1280]{4,0,3,1,2:T(4,128)(2,1)}), bf16[3,1,16,9,1280]{4,0,3,1,2:T(4,128)(2,1)S(1)}, u32[]{:S(2)}, u32[]{:S(2)}) async-start(bf16[3,1,16,9,1280]{4,0,3,1,2:T(4,128)(2,1)} %bitcast.83), calls=%async_computation.1 | async-start | bytes 2949120 | tf_op jit(solution)/shard_map/all_to_all | solution.py:123
  217.1 36.5 %all-to-all-done.1 = bf16[3,1,16,9,1280]{4,0,3,1,2:T(4,128)(2,1)S(1)} async-done(((bf16[3,1,16,9,1280]{4,0,3,1,2:T(4,128)(2,1)}), bf16[3,1,16,9,1280]{4,0,3,1,2:T(4,128)(2,1)S(1)}, u32[]{:S(2)}, u32[]{:S(2)}) %all-to-all-start.1) | async-done | bytes 1105952 | tf_op jit(solution)/shard_map/all_to_all | solution.py:123
  253.6 6.3 %slice_reduce_fusion.2 = (bf16[16,9,1280]{2,1,0:T(8,128)(2,1)S(1)}, bf16[16,9,1280]{2,1,0:T(8,128)(2,1)}, bf16[16,9,1280]{2,1,0:T(8,128)(2,1)}) fusion(bf16[3,1,16,9,1280]{4,0,3,1,2:T(4,128)(2,1)S(1)} %all-to-all-done.1), kind=kLoop, calls=%fused_computation.43 | loop fusion | bytes 2211840 | tf_op jit(solution)/shard_map/slice | solution.py:124
  259.9 1.8 reshape.221
  261.7 2.5 reshape.222
  264.2 1.6 reshape.220
  265.8 3.2 fusion.56
  268.9 2.1 fusion.26
  271.8 29.5 %all_to_all.30 = bf16[16,1,9,1280]{3,2,1,0:T(8,128)(2,1)S(1)} all-to-all(bf16[16,1,9,1280]{3,2,1,0:T(8,128)(2,1)S(1)} %reshape.223), channel_id=1, replica_groups=mesh['view'=16,'chip'=8,'core'=2] {'view'}, dimensions={0} | all-to-all | bytes 737280 | tf_op jit(solution)/shard_map/all_to_all | solution.py:37
  301.3 10.7 %all-gather.11.cloned.1.call-done = bf16[1280,640]{1,0:T(8,128)(2,1)} async-done(((bf16[80,640]{1,0:T(8,128)(2,1)}), bf16[1280,640]{1,0:T(8,128)(2,1)}) %all-gather.11.cloned.1.call-update) | async-done | bytes 1638416 | tf_op jit(solution)/shard_map/all_gather | solution.py:122
  312.7 20.9 %all-gather.17.cloned.1.call-done = bf16[2560,640]{1,0:T(8,128)(2,1)} async-done(((bf16[1280,640]{1,0:T(8,128)(2,1)}), bf16[2560,640]{1,0:T(8,128)(2,1)}) %all-gather.17.cloned.1.call-update) | async-done | bytes 3276816 | tf_op jit(solution)/shard_map/all_gather | solution.py:126
  333.6 5.7 %copy.99 = bf16[2,1280,640]{1,2,0:T(8,128)(2,1)} copy(bf16[2,1280,640]{2,1,0:T(8,128)(2,1)} %bitcast.88) | data formatting | bytes 6553600 | tf_op jit(solution)/shard_map/all_gather | solution.py:126
  339.3 3.9 %fusion.19 = bf16[1,1,2,72,1280]{4,3,2,1,0:T(8,128)(2,1)} fusion(f32[2,72,1280]{2,1,0:T(8,128)S(1)} %reshape.198, bf16[2,72,1280]{2,1,0:T(8,128)(2,1)S(1)} %dot_general.29, bf16[1280,1280,1]{1,0,2:T(8,128)(2,1)} %bitcast.79), kind=kOutput, calls=%fused_computation.24 | convolution fusion | flops 472227840 | bytes 4751360 | tf_op jit(solution)/shard_map/pc,kcd->pkd/dot_general | solution.py:131
  (73 shorter events, 11.8 us)
Async XLA Ops:
  6.5 87.4 %copy-start = (bf16[3,3,1280,80]{2,3,1,0:T(8,128)(2,1)S(1)}, bf16[3,3,1280,80]{2,3,1,0:T(8,128)(2,1)}, u32[]{:S(2)}) copy-start(bf16[3,3,1280,80]{2,3,1,0:T(8,128)(2,1)} %param.20) | copy-start | bytes 5529604
  6.5 50.4 %all-gather.9.cloned.1.call-start = ((), (), s32[]{:S(2)}) async-start(), calls=%async_computation.3 | async-start | bytes 6266880 | tf_op jit(solution)/shard_map/all_gather | solution.py:58
  7.3 154.9 %all-gather.13.cloned.1.call-start = ((), (), s32[]{:S(2)}) async-start(), calls=%async_computation.5 | async-start | bytes 5222400 | tf_op jit(solution)/shard_map/all_gather | solution.py:64
  58.7 133.1 %all-gather.15.cloned.1.call-start = ((), (), s32[]{:S(2)}) async-start(), calls=%async_computation.6 | async-start | bytes 14745600 | tf_op jit(solution)/shard_map/all_gather | solution.py:102
  61.2 13.4 %slice-start = ((s8[5898240]{0:T(1024)(128)(4,1)}), s8[1703936]{0:T(1024)(128)(4,1)S(1)}, s32[]{:S(2)}) async-start(s8[5898240]{0:T(1024)(128)(4,1)} %bitcast.76), calls=%async_computation.8 | async-start | bytes 3407872
  67.9 6.8 %slice-start.1 = ((s8[5898240]{0:T(1024)(128)(4,1)}), s8[4194304]{0:T(1024)(128)(4,1)S(1)}, s32[]{:S(2)}) async-start(s8[5898240]{0:T(1024)(128)(4,1)} %bitcast.76), calls=%async_computation.9 | async-start | bytes 8388608
  75.5 5.3 %copy-start.3 = (f32[1280]{0:T(1024)S(1)}, f32[1280]{0:T(1024)}, u32[]{:S(2)}) copy-start(f32[1280]{0:T(1024)} %get-tuple-element.26) | copy-start | bytes 15364
  75.5 5.3 %copy-start.4 = (f32[1280]{0:T(1024)S(1)}, f32[1280]{0:T(1024)}, u32[]{:S(2)}) copy-start(f32[1280]{0:T(1024)} %get-tuple-element.27) | copy-start | bytes 15364
  75.5 5.3 %copy-start.6 = (f32[1280]{0:T(1024)S(1)}, f32[1280]{0:T(1024)}, u32[]{:S(2)}) copy-start(f32[1280]{0:T(1024)} %param.15) | copy-start | bytes 15364
  75.5 5.3 %copy-start.7 = (f32[1280]{0:T(1024)S(1)}, f32[1280]{0:T(1024)}, u32[]{:S(2)}) copy-start(f32[1280]{0:T(1024)} %param.14) | copy-start | bytes 15364
  89.9 4.0 %copy-start.10 = (pred[8,10]{0,1:T(8,128)(4,1)S(1)}, pred[8,10]{0,1:T(8,128)(4,1)}, u32[]{:S(2)}) copy-start(pred[8,10]{0,1:T(8,128)(4,1)} %constant.46) | copy-start | bytes 244
  93.9 17.5 %copy-start.8 = (f32[80]{0:T(128)S(1)}, f32[80]{0:T(128)}, u32[]{:S(2)}) copy-start(f32[80]{0:T(128)} %dynamic_slice.14) | copy-start | bytes 964
  111.4 59.9 %copy-start.5 = (f32[1280]{0:T(1024)S(1)}, f32[1280]{0:T(1024)}, u32[]{:S(2)}) copy-start(f32[1280]{0:T(1024)} %param.22) | copy-start | bytes 15364
  111.4 60.0 %copy-start.2 = (bf16[80,1280]{1,0:T(8,128)(2,1)S(1)}, bf16[80,1280]{1,0:T(8,128)(2,1)}, u32[]{:S(2)}) copy-start(bf16[80,1280]{1,0:T(8,128)(2,1)} %param.24) | copy-start | bytes 614404
  163.2 18.1 %all-to-all-start = ((bf16[1,1,32,72,80]{4,3,1,0,2:T(8,128)(2,1)}), bf16[1,1,32,72,80]{4,3,1,0,2:T(8,128)(2,1)S(1)}, u32[]{:S(2)}, u32[]{:S(2)}) async-start(bf16[1,1,32,72,80]{4,3,1,0,2:T(8,128)(2,1)} %copy.84), calls=%async_computation | async-start | bytes 1179648 | tf_op jit(solution)/shard_map/all_to_all | solution.py:103
  200.1 17.0 %copy-start.9 = (f32[20]{0:T(128)S(1)}, f32[20]{0:T(128)}, u32[]{:S(2)}) copy-start(f32[20]{0:T(128)} %param.25) | copy-start | bytes 244
  207.5 46.2 %all-to-all-start.1 = ((bf16[3,1,16,9,1280]{4,0,3,1,2:T(4,128)(2,1)}), bf16[3,1,16,9,1280]{4,0,3,1,2:T(4,128)(2,1)S(1)}, u32[]{:S(2)}, u32[]{:S(2)}) async-start(bf16[3,1,16,9,1280]{4,0,3,1,2:T(4,128)(2,1)} %bitcast.83), calls=%async_computation.1 | async-start | bytes 2949120 | tf_op jit(solution)/shard_map/all_to_all | solution.py:123
  216.5 95.5 %all-gather.11.cloned.1.call-start = ((), (), s32[]{:S(2)}) async-start(), calls=%async_computation.4 | async-start | bytes 1740800 | tf_op jit(solution)/shard_map/all_gather | solution.py:122
  217.1 116.5 %all-gather.17.cloned.1.call-start = ((), (), s32[]{:S(2)}) async-start(), calls=%async_computation.7 | async-start | bytes 4915200 | tf_op jit(solution)/shard_map/all_gather | solution.py:126
  333.6 9.6 %copy-start.1 = (bf16[3,3,1280,80]{2,3,1,0:T(8,128)(2,1)S(1)}, bf16[3,3,1280,80]{2,3,1,0:T(8,128)(2,1)}, u32[]{:S(2)}) copy-start(bf16[3,3,1280,80]{2,3,1,0:T(8,128)(2,1)} %param.20) | copy-start | bytes 5529604
Sparse Core Ops, SparseCore 0:
  9.2 47.7 all-gather.8
  59.6 102.5 all-gather.12
  164.0 27.7 all-gather.14
  219.6 92.3 all-gather.10
  313.7 19.8 all-gather.16

commit v3 on v2

--- a/solution.py
+++ b/solution.py
@@ -34,7 +34,7 @@
 
 
 def send_back(mixed):
-    return lax.all_to_all(mixed, "view", split_axis=0, concat_axis=1, tiled=True)
+    return lax.all_to_all(mixed, VIEW, split_axis=0, concat_axis=1, tiled=True)
 
 
 def local(
@@ -61,7 +61,8 @@
     half_in = attn_in.shape[1] // 2
     half_out = attn_out.shape[1] // 2
     in_half = lax.dynamic_slice_in_dim(attn_in, core * half_in, half_in, axis=1)
-    in_half = lax.all_gather(in_half, "view", axis=0, tiled=False)
+    in_half = lax.all_gather(in_half, "vz", axis=0, tiled=False)
+    in_half = lax.all_gather(in_half, "vy", axis=0, tiled=False)
     out_half = lax.dynamic_slice_in_dim(attn_out, core * half_out, half_out, axis=1)
 
     all_rows = whole.shape[2]
@@ -99,7 +100,8 @@
     latent_part = lax.dynamic_slice_in_dim(whole, me * out_part, out_part, axis=4)
     resid_part = (latent_part.astype(jnp.float32) + conv_out + bias_part).astype(jnp.bfloat16)
     in_half, resid_part = lax.optimization_barrier((in_half, resid_part))
-    weights_in = lax.all_gather(in_half, "core", axis=0, tiled=False)
+    swap = [(0, 1), (1, 0)]
+    in_other = lax.ppermute(in_half, "core", swap)
     resid_out = lax.all_to_all(resid_part, ROW, split_axis=2, concat_axis=4, tiled=True)
     resid_float = resid_out.astype(jnp.float32)
     middle = jnp.mean(resid_float, axis=-1, keepdims=True)
@@ -107,61 +109,78 @@
     normed_y = ((resid_float - middle) * lax.rsqrt(spread_y + epsilon) * ln_gain).astype(
         jnp.bfloat16
     )
-    view_devices = lax.axis_size("view")
+    view_devices = lax.axis_size(VIEW)
     per_device = samples * local_rows * local_cols // view_devices
     pixel_major = jnp.moveaxis(normed_y, 1, 0).reshape(
         local_views, view_devices, per_device, width_out
     )
 
-    flat_block = pixel_major.reshape(-1, 2, width_out // 2)
+    flat_block = pixel_major.reshape(-1, width_out)
+    block_mine = lax.dynamic_slice_in_dim(flat_block, core * half_in, half_in, axis=1)
+    block_other = lax.dynamic_slice_in_dim(flat_block, (1 - core) * half_in, half_in, axis=1)
     triple_in = jnp.einsum(
-        "pkc,kjmcd->mpjd", flat_block, weights_in, preferred_element_type=jnp.float32
-    ).astype(jnp.bfloat16)
+        "pc,yzmcd->mpzyd", block_mine, in_half, preferred_element_type=jnp.float32
+    ) + jnp.einsum(
+        "pc,yzmcd->mpzyd", block_other, in_other, preferred_element_type=jnp.float32
+    )
+    triple_in = triple_in.astype(jnp.bfloat16)
     triple_in = triple_in.reshape((3,) + pixel_major.shape)
     out_half, triple_in = lax.optimization_barrier((out_half, triple_in))
-    out_half = lax.all_gather(out_half, "view", axis=0, tiled=True)
-    triple_in = lax.all_to_all(triple_in, "view", split_axis=2, concat_axis=1, tiled=True)
+    out_half = lax.all_gather(out_half, "vz", axis=0, tiled=False)
+    out_half = lax.all_gather(out_half, "vy", axis=0, tiled=False)
+    triple_in = lax.all_to_all(triple_in, VIEW, split_axis=2, concat_axis=1, tiled=True)
     mixed = send_back(attend(triple_in[0], triple_in[1], triple_in[2], head_scale))
     out_half, mixed = lax.optimization_barrier((out_half, mixed))
-    weights_out = lax.all_gather(out_half, "core", axis=0, tiled=False)
+    out_other = lax.ppermute(out_half, "core", swap)
     mixed = jnp.moveaxis(
         mixed.reshape(local_views, samples, local_rows, local_cols, width_out), 0, 1
     )
-    flat_mixed = mixed.reshape(-1, width_out)
-    projected = jnp.einsum(
-        "pc,kcd->pkd", flat_mixed, weights_out, preferred_element_type=jnp.float32
+    flat_mixed = mixed.reshape(-1, lax.axis_size("vz"), lax.axis_size("vy"), out_half.shape[2])
+    cols_mine = jnp.einsum(
+        "pzyr,yzrd->pd", flat_mixed, out_half, preferred_element_type=jnp.float32
+    )
+    cols_other = jnp.einsum(
+        "pzyr,yzrd->pd", flat_mixed, out_other, preferred_element_type=jnp.float32
+    )
+    projected = jnp.where(
+        core == 0,
+        jnp.concatenate([cols_mine, cols_other], axis=1),
+        jnp.concatenate([cols_other, cols_mine], axis=1),
     )
     return (resid_float + projected.reshape(resid_float.shape)).astype(jnp.bfloat16)
 
 
 ROW = ("chip", "core")
+VIEW = ("vz", "vy")
 
 
 def solution(mesh):
     cores = 2
     split = jax.sharding.Mesh(
-        mesh.devices.reshape(mesh.shape["view"], mesh.shape["row"] // cores, cores),
-        ("view", "chip", "core"),
+        mesh.devices.reshape(
+            mesh.shape["view"] // 2, 2, mesh.shape["row"] // cores, cores
+        ),
+        ("vz", "vy", "chip", "core"),
     )
     placed = (
-        P(None, "view", ROW, None, None),
+        P(None, VIEW, ROW, None, None),
         P(),
         P(),
-        P(None, "view"),
+        P(None, VIEW),
         P(),
         P(),
         P(),
         P(None, None, None, ROW),
         P(),
         P(),
-        P(None, None, "view"),
-        P("view", None),
+        P(None, None, VIEW),
+        P(VIEW, None),
         P(),
     )
     return jax.shard_map(
         local,
         mesh=split,
         in_specs=placed,
-        out_specs=P(None, "view", ROW, None, None),
+        out_specs=P(None, VIEW, ROW, None, None),
         check_vma=False,
     )

time: 357 us -> 348 us (0.975)
  waiting for transfers between devices: 184 us -> 136 us
  blocking collectives: 29.5 us -> 52.7 us
  starting transfers between devices: 17.3 us -> 27.8 us
    all_gather x0 -> x1, blocking collectives: none -> 52.7 us  [local(): out_half = lax.all_gather(out_half, 'vz', axis=0, tiled=False)]
    all_to_all x1 -> x2, waiting for transfers between devices: 36.5 us -> 0.01 us  [the longest x1 0.01 us: local(): lax.all_to_all(triple_in, VIEW, split_axis=2, concat_axis=1, tiled=True)]
    all_to_all x1 -> x0, blocking collectives: 29.5 us -> none  [send_back(): lax.all_to_all(mixed, 'view', split_axis=0, concat_axis=1, tiled=True)]
    all_gather x4 -> x3, waiting for transfers between devices: 86.9 us -> 75.7 us  [the longest x1 42.6 us: local(): in_half = lax.all_gather(in_half, 'vy', axis=0, tiled=False)]
    all_to_all x1 -> x2, starting transfers between devices: 9.02 us -> 16.3 us  [the longest x1 8.31 us: local(): lax.all_to_all(triple_in, VIEW, split_axis=2, concat_axis=1, tiled=True)]
    ppermute x0 -> x2, starting transfers between devices: none -> 6.72 us  [the longest x1 6.05 us: local(): out_other = lax.ppermute(out_half, 'core', swap)]
    all_gather x1 -> x0, local copies, waits for them, and re-layouts: 5.72 us -> none  [local(): weights_out = lax.all_gather(out_half, 'core', axis=0, tiled=False)]
    dot_general x2 -> x4, matrix products: 12.1 us -> 14.3 us  [the longest x1 5.16 us: local(): jnp.einsum('pc,yzmcd->mpzyd', block_other, in_other, preferred_element_ty...]
  transfers between devices with their start and end apart: 7 -> 9, of which waited for: 7 -> 5; matrix products, arithmetic and copies ran while one was open for 22% -> 26% of each run, Pallas kernels for 0% -> 0%
where the time goes in v3:
time: 348 us; the launch traced here: 342 us
  waiting for transfers between devices  136 us (39%)
  blocking collectives  52.7 us (15%)
  local copies, waits for them, and re-layouts  48.8 us (14%)
  matrix products  40.1 us (12%)
  starting transfers between devices  27.8 us (8%)
  other arithmetic  21 us (6%)
  between operations  15.3 us (4%)
    all_gather x1, blocking collectives, local(): out_half = lax.all_gather(out_half, 'vz', axis=0, tiled=False)  52.7 us
    all_gather x1, waiting for transfers between devices, local(): whole = lax.all_gather(latent, ROW, axis=2, tiled=True)  49.7 us
    all_gather x1, waiting for transfers between devices, local(): in_half = lax.all_gather(in_half, 'vy', axis=0, tiled=False)  42.6 us
    conv_general_dilated x1, matrix products, local(): lax.conv_general_dilated(activated.reshape(samples * local_views, all_row...  17 us
    all_gather x1, waiting for transfers between devices, local(): in_half = lax.all_gather(in_half, 'vz', axis=0, tiled=False)  16.7 us
    all_gather x1, waiting for transfers between devices, local(): out_half = lax.all_gather(out_half, 'vy', axis=0, tiled=False)  16.3 us
    all_to_all x1, waiting for transfers between devices, local(): lax.all_to_all(resid_part, ROW, split_axis=2, concat_axis=4, tiled=True)  10 us
    reshape x1, other arithmetic, local(): activated.reshape(samples * local_views, all_rows, local_cols, channels)  8.6 us
  transfers between devices with their start and end apart: 9, of which 5 were waited for; matrix products, arithmetic and copies ran while one was open for 26% of the time, Pallas kernels for 0%

profile of v3, /device:TPU:1, one launch (start us, length us, event | category | flops | bytes accessed | tf_op | source)
XLA Modules:
  0.0 341.8 jit_solution(358484809918014826)
XLA Ops:
  7.3 49.7 %all-gather.9.cloned.1.call-done = bf16[1,1,32,72,1280]{4,3,1,0,2:T(8,128)(2,1)} async-done(((bf16[1,1,2,72,1280]{4,3,1,0,2:T(8,128)(2,1)}), bf16[1,1,32,72,1280]{4,3,1,0,2:T(8,128)(2,1)}) %all-gather.9.cloned.1.call-update) | async-done | bytes 5898256 | tf_op jit(solution)/shard_map/all_gather | solution.py:58
  57.0 1.7 constant_dynamic-slice_fusion.1
  61.2 3.4 convolution_reduce_fusion
  67.9 6.8 %copy.57 = bf16[1,1,32,72,1280]{4,2,3,1,0:T(8,128)(2,1)} copy(bf16[1,1,32,72,1280]{4,3,1,0,2:T(8,128)(2,1)} %all-gather.9.cloned.1.call-done) | data formatting | bytes 11796480 | tf_op jit(solution)/shard_map/optimization_barrier | solution.py:59
  76.0 4.5 %fusion.4 = f32[1280]{0:T(1024)S(1)} fusion(f32[1280]{0:T(1024)S(1)} %sub.51, bf16[1,1,32,72,1280]{4,3,1,0,2:T(8,128)(2,1)} %all-gather.9.cloned.1.call-done), kind=kLoop, calls=%fused_computation.7 | loop fusion | flops 11795200 | bytes 5908480 | tf_op jit(solution)/shard_map/reduce_sum | solution.py:75
  80.9 16.7 %all-gather.11.cloned.1.call-done = bf16[24,640,80]{1,2,0:T(8,128)(2,1)} async-done(((bf16[3,640,80]{1,2,0:T(8,128)(2,1)}), bf16[24,640,80]{1,2,0:T(8,128)(2,1)}) %all-gather.11.cloned.1.call-update) | async-done | bytes 2457616 | tf_op jit(solution)/shard_map/all_gather | solution.py:64
  97.6 8.6 %fusion.16 = bf16[32,1,72,1280]{3,0,2,1:T(8,128)(2,1)S(1)} fusion(f32[1280]{0:T(1024)S(1)} %copy-done.5, f32[1280]{0:T(1024)S(1)} %copy-done.4, f32[1280]{0:T(1024)S(1)} %copy-done.7, f32[1280]{0:T(1024)S(1)} %copy-done.8, f32[1280]{0:T(1024)S(1)} %mul.98, f32[1280]{0:T(1024)S(1)} %sub.51, bf16[1,1,32,72,1280]{4,3,1,0,2:T(8,128)(2,1)} %all-gather.9.cloned.1.call-done), kind=kLoop, calls=%fused_computation.19 | loop fusion | flops 35389440 | bytes 11827200 | tf_op jit(solution)/shard_map/reshape | solution.py:91
  107.1 3.6 %copy.60 = bf16[32,1,8,10,1280]{4,2,3,0,1:T(8,128)(2,1)S(1)} copy(bf16[32,1,8,10,1280]{4,0,3,2,1:T(8,128)(2,1)S(1)} %bitcast.92) | data formatting | bytes 13107200 | tf_op jit(solution)/shard_map/conv_general_dilated | solution.py:90
  111.1 17.0 %fusion.25 = f32[32,8,10,80]{3,1,2,0:T(8,128)S(1)} fusion(bf16[3,3,1280,80]{2,3,1,0:T(8,128)(2,1)S(1)} %copy-done, bf16[32,1,7,2,1280]{4,2,3,0,1:T(8,128)(2,1)S(1)} %slice.28, bf16[32,1,8,10,1280]{4,2,3,0,1:T(8,128)(2,1)S(1)} %copy.60, pred[8,10]{0,1:T(8,128)(4,1)S(1)} %copy-done.11), kind=kOutput, calls=%fused_computation.32 | convolution fusion | flops 4644085760 | bytes 10362960 | tf_op jit(solution)/shard_map/conv_general_dilated | solution.py:90
  128.5 1.6 fusion.37
  130.1 42.6 %all-gather.13.cloned.1.call-done = bf16[16,3,640,80]{2,3,1,0:T(8,128)(2,1)} async-done(((bf16[8,3,640,80]{2,3,1,0:T(8,128)(2,1)}), bf16[16,3,640,80]{2,3,1,0:T(8,128)(2,1)}) %all-gather.13.cloned.1.call-update) | async-done | bytes 4915216 | tf_op jit(solution)/shard_map/all_gather | solution.py:65
  174.5 4.7 %all-to-all-start = ((bf16[1,1,32,72,80]{4,3,1,0,2:T(8,128)(2,1)}), bf16[1,1,32,72,80]{4,3,1,0,2:T(8,128)(2,1)S(1)}, u32[]{:S(2)}, u32[]{:S(2)}) async-start(bf16[1,1,32,72,80]{4,3,1,0,2:T(8,128)(2,1)} %copy.62), calls=%async_computation | async-start | bytes 1179648 | tf_op jit(solution)/shard_map/all_to_all | solution.py:105
  179.2 10.0 %all-to-all-done = bf16[1,1,32,72,80]{4,3,1,0,2:T(8,128)(2,1)S(1)} async-done(((bf16[1,1,32,72,80]{4,3,1,0,2:T(8,128)(2,1)}), bf16[1,1,32,72,80]{4,3,1,0,2:T(8,128)(2,1)S(1)}, u32[]{:S(2)}, u32[]{:S(2)}) %all-to-all-start) | async-done | bytes 368672 | tf_op jit(solution)/shard_map/all_to_all | solution.py:105
  190.2 2.0 multiply_reduce_fusion
  193.0 5.1 %fusion.47 = f32[2,8,3,80,144]{3,4,2,1,0:T(8,128)S(1)} fusion(bf16[2,8,3,640,80]{3,4,2,1,0:T(8,128)(2,1)} %bitcast.94, bf16[144,1280]{1,0:T(8,128)(2,1)S(1)} %multiply_convert_fusion.1, s32[]{:T(128)S(6)} %select_n.28), kind=kOutput, calls=%fused_computation.58 | convolution fusion | flops 707788800 | bytes 7311364 | tf_op jit(solution)/shard_map/pc,yzmcd->mpzyd/dot_general | solution.py:121
  198.1 5.2 %fusion.23 = bf16[3,144,8,2,80]{4,1,0,2,3:T(8,128)(2,1)S(1)} fusion(f32[2,8,3,80,144]{3,4,2,1,0:T(8,128)S(1)} %fusion.47, bf16[2,8,3,640,80]{3,4,2,1,0:T(8,128)(2,1)} %collective-permute-done, bf16[144,1280]{1,0:T(8,128)(2,1)S(1)} %multiply_convert_fusion.1, s32[]{:T(128)S(6)} %select_n.31), kind=kOutput, calls=%fused_computation.27 | convolution fusion | flops 708894720 | bytes 9744388 | tf_op jit(solution)/shard_map/pc,yzmcd->mpzyd/dot_general | solution.py:123
  203.3 3.0 copy.64
  206.3 8.5 %reshape.273 = bf16[3,1,16,9,1280]{4,0,3,2,1:T(4,128)(2,1)} reshape(bf16[3,144,8,2,80]{4,3,2,0,1:T(2,128)(2,1)} %copy.64) | data formatting | bytes 2211840 | tf_op jit(solution)/shard_map/reshape | solution.py:127
  214.8 8.3 %all-to-all-start.1 = ((bf16[3,1,16,9,1280]{4,0,3,1,2:T(4,128)(2,1)}), bf16[3,1,16,9,1280]{4,0,3,1,2:T(4,128)(2,1)S(1)}, u32[]{:S(2)}, u32[]{:S(2)}) async-start(bf16[3,1,16,9,1280]{4,0,3,1,2:T(4,128)(2,1)} %bitcast.97), calls=%async_computation.1 | async-start | bytes 2949120 | tf_op jit(solution)/shard_map/all_to_all | solution.py:131
  223.2 52.7 %all-gather.2 = bf16[640,640]{1,0:T(8,128)(2,1)} all-gather(bf16[80,640]{1,0:T(8,128)(2,1)S(1)} %constant_dynamic-slice_fusion), channel_id=4, replica_groups=mesh['vz'=8,'vy'=2,'chip'=8,'core'=2] {'vz'}, dimensions={0}, use_global_device_ids=true | all-gather | bytes 921600 | tf_op jit(solution)/shard_map/all_gather | solution.py:129
  276.0 6.5 %slice_reduce_fusion.2 = (bf16[16,9,1280]{2,1,0:T(8,128)(2,1)}, bf16[16,9,1280]{2,1,0:T(8,128)(2,1)}, bf16[16,9,1280]{2,1,0:T(8,128)(2,1)}) fusion(bf16[3,1,16,9,1280]{4,0,3,1,2:T(4,128)(2,1)S(1)} %all-to-all-done.1), kind=kLoop, calls=%fused_computation.46 | loop fusion | bytes 2211840 | tf_op jit(solution)/shard_map/slice | solution.py:132
  282.5 1.8 reshape.310
  284.3 1.8 reshape.311
  286.0 2.5 reshape.309
  288.5 2.0 fusion.66
  290.5 2.3 fusion.28
  294.4 8.0 %all-to-all-start.2 = ((bf16[16,1,9,1280]{3,2,1,0:T(8,128)(2,1)}), bf16[16,1,9,1280]{3,2,1,0:T(8,128)(2,1)}, u32[]{:S(2)}, u32[]{:S(2)}) async-start(bf16[16,1,9,1280]{3,2,1,0:T(8,128)(2,1)} %reshape.312), calls=%async_computation.2 | async-start | bytes 1310720 | tf_op jit(solution)/shard_map/all_to_all | solution.py:37
  302.4 16.3 %all-gather.15.cloned.1.call-done = bf16[16,80,640]{2,1,0:T(8,128)(2,1)} async-done(((bf16[8,80,640]{2,1,0:T(8,128)(2,1)}), bf16[16,80,640]{2,1,0:T(8,128)(2,1)}) %all-gather.15.cloned.1.call-update) | async-done | bytes 1638416 | tf_op jit(solution)/shard_map/all_gather | solution.py:130
  318.7 6.0 %collective-permute-start.1 = (bf16[2,8,80,640]{3,2,1,0:T(8,128)(2,1)}, bf16[2,8,80,640]{3,2,1,0:T(8,128)(2,1)}, u32[]{:S(2)}, u32[]{:S(2)}) collective-permute-start(bf16[2,8,80,640]{3,2,1,0:T(8,128)(2,1)} %bitcast.107), channel_id=1, source_target_pairs={{0,1},{1,0},{2,3},{3,2},{4,5},{5,4},{6,7},{7,6},{8,9},{9,8},{10,11... | collective-permute-start | bytes 4915208 | tf_op jit(solution)/shard_map/ppermute | solution.py:134
  326.1 3.6 %reshape_transpose_reshape.3 = bf16[144,8,2,80]{3,2,1,0:T(2,128)(2,1)S(1)} reshape(bf16[1,16,9,1280]{3,2,1,0:T(8,128)(2,1)} %bitcast.22) | data formatting | bytes 737280 | tf_op jit(solution)/shard_map/reshape;transpose;reshape | solution.py:138
  329.8 2.1 fusion.29
  331.9 2.1 fusion.32
  (80 shorter events, 16.0 us)
Async XLA Ops:
  6.5 104.5 %copy-start = (bf16[3,3,1280,80]{2,3,1,0:T(8,128)(2,1)S(1)}, bf16[3,3,1280,80]{2,3,1,0:T(8,128)(2,1)}, u32[]{:S(2)}) copy-start(bf16[3,3,1280,80]{2,3,1,0:T(8,128)(2,1)} %param.20) | copy-start | bytes 5529604
  6.5 50.4 %all-gather.9.cloned.1.call-start = ((), (), s32[]{:S(2)}) async-start(), calls=%async_computation.3 | async-start | bytes 6266880 | tf_op jit(solution)/shard_map/all_gather | solution.py:58
  7.3 90.3 %all-gather.11.cloned.1.call-start = ((), (), s32[]{:S(2)}) async-start(), calls=%async_computation.4 | async-start | bytes 2764800 | tf_op jit(solution)/shard_map/all_gather | solution.py:64
  58.7 114.0 %all-gather.13.cloned.1.call-start = ((), (), s32[]{:S(2)}) async-start(), calls=%async_computation.5 | async-start | bytes 7372800 | tf_op jit(solution)/shard_map/all_gather | solution.py:65
  61.2 13.5 %slice-start = ((s8[5898240]{0:T(1024)(128)(4,1)}), s8[1703936]{0:T(1024)(128)(4,1)S(1)}, s32[]{:S(2)}) async-start(s8[5898240]{0:T(1024)(128)(4,1)} %bitcast.90), calls=%async_computation.7 | async-start | bytes 3407872
  67.8 6.8 %slice-start.1 = ((s8[5898240]{0:T(1024)(128)(4,1)}), s8[4194304]{0:T(1024)(128)(4,1)S(1)}, s32[]{:S(2)}) async-start(s8[5898240]{0:T(1024)(128)(4,1)} %bitcast.90), calls=%async_computation.8 | async-start | bytes 8388608
  75.6 22.0 %copy-start.4 = (f32[1280]{0:T(1024)S(1)}, f32[1280]{0:T(1024)}, u32[]{:S(2)}) copy-start(f32[1280]{0:T(1024)} %get-tuple-element.26) | copy-start | bytes 15364
  75.6 22.0 %copy-start.5 = (f32[1280]{0:T(1024)S(1)}, f32[1280]{0:T(1024)}, u32[]{:S(2)}) copy-start(f32[1280]{0:T(1024)} %get-tuple-element.27) | copy-start | bytes 15364
  75.6 22.0 %copy-start.7 = (f32[1280]{0:T(1024)S(1)}, f32[1280]{0:T(1024)}, u32[]{:S(2)}) copy-start(f32[1280]{0:T(1024)} %param.15) | copy-start | bytes 15364
  75.6 22.0 %copy-start.8 = (f32[1280]{0:T(1024)S(1)}, f32[1280]{0:T(1024)}, u32[]{:S(2)}) copy-start(f32[1280]{0:T(1024)} %param.14) | copy-start | bytes 15364
  107.1 4.0 %copy-start.11 = (pred[8,10]{0,1:T(8,128)(4,1)S(1)}, pred[8,10]{0,1:T(8,128)(4,1)}, u32[]{:S(2)}) copy-start(pred[8,10]{0,1:T(8,128)(4,1)} %constant.48) | copy-start | bytes 244
  111.1 17.4 %copy-start.9 = (f32[80]{0:T(128)S(1)}, f32[80]{0:T(128)}, u32[]{:S(2)}) copy-start(f32[80]{0:T(128)} %dynamic_slice.20) | copy-start | bytes 964
  128.0 51.1 %copy-start.3 = (bf16[80,1280]{1,0:T(8,128)(2,1)S(1)}, bf16[80,1280]{1,0:T(8,128)(2,1)}, u32[]{:S(2)}) copy-start(bf16[80,1280]{1,0:T(8,128)(2,1)} %param.24) | copy-start | bytes 614404
  172.7 20.1 %copy-start.6 = (f32[1280]{0:T(1024)S(1)}, f32[1280]{0:T(1024)}, u32[]{:S(2)}) copy-start(f32[1280]{0:T(1024)} %param.22) | copy-start | bytes 15364
  172.7 25.4 %collective-permute-start = (bf16[2,8,3,640,80]{3,4,2,1,0:T(8,128)(2,1)}, bf16[2,8,3,640,80]{3,4,2,1,0:T(8,128)(2,1)}, u32[]{:S(2)}, u32[]{:S(2)}) collective-permute-start(bf16[2,8,3,640,80]{3,4,2,1,0:T(8,128)(2,1)} %bitcast.93), channel_id=1, source_target_pairs={{0,1},{1,0},{2,3},{3,2},{4,5},{5,4},{6,7},{7,6},{8,9},{9,8},{10,11... | collective-permute-start | bytes 14745608 | tf_op jit(solution)/shard_map/ppermute | solution.py:104
  174.5 14.8 %all-to-all-start = ((bf16[1,1,32,72,80]{4,3,1,0,2:T(8,128)(2,1)}), bf16[1,1,32,72,80]{4,3,1,0,2:T(8,128)(2,1)S(1)}, u32[]{:S(2)}, u32[]{:S(2)}) async-start(bf16[1,1,32,72,80]{4,3,1,0,2:T(8,128)(2,1)} %copy.62), calls=%async_computation | async-start | bytes 1179648 | tf_op jit(solution)/shard_map/all_to_all | solution.py:105
  203.3 19.9 %copy-start.10 = (f32[20]{0:T(128)S(1)}, f32[20]{0:T(128)}, u32[]{:S(2)}) copy-start(f32[20]{0:T(128)} %param.25) | copy-start | bytes 244
  214.8 61.2 %all-to-all-start.1 = ((bf16[3,1,16,9,1280]{4,0,3,1,2:T(4,128)(2,1)}), bf16[3,1,16,9,1280]{4,0,3,1,2:T(4,128)(2,1)S(1)}, u32[]{:S(2)}, u32[]{:S(2)}) async-start(bf16[3,1,16,9,1280]{4,0,3,1,2:T(4,128)(2,1)} %bitcast.97), calls=%async_computation.1 | async-start | bytes 2949120 | tf_op jit(solution)/shard_map/all_to_all | solution.py:131
  223.1 95.6 %all-gather.15.cloned.1.call-start = ((), (), s32[]{:S(2)}) async-start(), calls=%async_computation.6 | async-start | bytes 2457600 | tf_op jit(solution)/shard_map/all_gather | solution.py:130
  294.4 24.3 %all-to-all-start.2 = ((bf16[16,1,9,1280]{3,2,1,0:T(8,128)(2,1)}), bf16[16,1,9,1280]{3,2,1,0:T(8,128)(2,1)}, u32[]{:S(2)}, u32[]{:S(2)}) async-start(bf16[16,1,9,1280]{3,2,1,0:T(8,128)(2,1)} %reshape.312), calls=%async_computation.2 | async-start | bytes 1310720 | tf_op jit(solution)/shard_map/all_to_all | solution.py:37
  318.7 13.1 %collective-permute-start.1 = (bf16[2,8,80,640]{3,2,1,0:T(8,128)(2,1)}, bf16[2,8,80,640]{3,2,1,0:T(8,128)(2,1)}, u32[]{:S(2)}, u32[]{:S(2)}) collective-permute-start(bf16[2,8,80,640]{3,2,1,0:T(8,128)(2,1)} %bitcast.107), channel_id=1, source_target_pairs={{0,1},{1,0},{2,3},{3,2},{4,5},{5,4},{6,7},{7,6},{8,9},{9,8},{10,11... | collective-permute-start | bytes 4915208 | tf_op jit(solution)/shard_map/ppermute | solution.py:134
  324.8 10.1 %copy-start.1 = (bf16[3,3,1280,80]{2,3,1,0:T(8,128)(2,1)S(1)}, bf16[3,3,1280,80]{2,3,1,0:T(8,128)(2,1)}, u32[]{:S(2)}) copy-start(bf16[3,3,1280,80]{2,3,1,0:T(8,128)(2,1)} %param.20) | copy-start | bytes 5529604
  326.1 7.8 %copy-start.2 = (f32[1,1,2,72,1280]{4,3,2,1,0:T(8,128)S(1)}, f32[1,1,2,72,1280]{4,3,2,1,0:T(8,128)}, u32[]{:S(2)}) copy-start(f32[1,1,2,72,1280]{4,3,2,1,0:T(8,128)} %reshape.283) | copy-start | bytes 2211844
Sparse Core Ops, SparseCore 0:
  9.2 47.7 all-gather.8
  58.8 38.6 all-gather.10
  99.4 73.3 all-gather.12
  276.1 42.6 all-gather.14
